TPU v7x, 1024 devices: a whole 4x4x32 slice. The times are simulated.
1024 devices in a mesh: fsdp: 32 (over z), ty: 4 (over y_lo, core), tx: 8 (over y_hi, x).
Axes of the slice: x: 4, y: 4 (y_hi: 2, y_lo: 2; y = y_hi * 2 + y_lo), z: 32, core: 2. Of those that a mesh axis runs over, the one named last changes fastest.
Arguments:
- q_raw: bfloat16 [64, 32, 64, 1536], P('fsdp', 'ty', 'tx'), may hold values from -6 to 6
- k_raw: bfloat16 [64, 32, 64, 1536], P('fsdp', 'ty', 'tx'), may hold values from -6 to 6
- values: bfloat16 [64, 32, 64, 1536], P('fsdp', 'ty', 'tx'), may hold values from -6 to 6
- d_out: bfloat16 [64, 32, 64, 1536], P('fsdp', 'ty', 'tx'), may hold values from -6 to 6
- q_gain: float32 [128], P('fsdp'), may hold values from 0.1 to 1.9
- k_gain: float32 [128], P('fsdp'), may hold values from 0.1 to 1.9
- windows: int32 [12, 2], replicated, may hold values from 1 to 3, as said below
Outputs:
- out: bfloat16 [64, 32, 64, 1536], P('fsdp', 'ty', 'tx')
- q_grad: bfloat16 [64, 32, 64, 1536], P('fsdp', 'ty', 'tx')
- k_grad: bfloat16 [64, 32, 64, 1536], P('fsdp', 'ty', 'tx')
- v_grad: bfloat16 [64, 32, 64, 1536], P('fsdp', 'ty', 'tx')
- q_gain_grad: float32 [128], P('fsdp')
- k_gain_grad: float32 [128], P('fsdp')
Inputs may be any that keep to these rules, and one draw needn't show every extreme that they name: `windows`: every entry is 1 or 3; in each of the two columns some head has 3.
All inputs are finite; a program needn't handle non-finite values.
Results may differ from a plain program's by a relative error of at most 0.0083.
Values may be sent and summed in bfloat16 or wider, within the bound.
No kernel may reach another device: no remote copies, remote signals or barrier semaphores. Data moves between devices by JAX's collectives and lax.ppermute only.
A program may use at most 64 MiB of HBM per device.

v0:
```python
import math

import jax
import jax.numpy as jnp
from jax import lax
from jax.sharding import PartitionSpec as P

TILE = 8


NORM_EPS = 1e-06


def padded(cells, sides, width):
    for axis, dim in sides:
        count = lax.axis_size(axis)
        ends = count - 1
        head = lax.slice_in_dim(cells, 0, width, axis=dim)
        tail = lax.slice_in_dim(cells, cells.shape[dim] - width, cells.shape[dim], axis=dim)
        cells = jnp.concatenate(
            [
                lax.ppermute(tail, axis, [(i, (i + 1) % count) for i in range(ends)]),
                cells,
                lax.ppermute(head, axis, [((i + 1) % count, i) for i in range(ends)]),
            ],
            axis=dim,
        )
    return cells


def xor_sum(cells, axis):
    count = lax.axis_size(axis)
    step = 1
    while step < count:
        cells = cells + lax.ppermute(cells, axis, [(i, i ^ step) for i in range(count)])
        step *= 2
    return cells


def product(form, left, right):
    return jnp.einsum(form, left, right, preferred_element_type=jnp.float32)


def normalize(raw_field, norm_gain, head_count):
    floats = raw_field.astype(jnp.float32)
    floats = floats.reshape(floats.shape[:-1] + (head_count, norm_gain.shape[0]))
    inverse = lax.rsqrt(jnp.mean(floats * floats, axis=-1, keepdims=True) + NORM_EPS)
    normed = floats * inverse
    return (normed, inverse, (normed * norm_gain).astype(jnp.bfloat16))


def norm_backward(upstream, normed, inverse, norm_gain):
    gain_part = jnp.sum(upstream * normed, axis=tuple(range(upstream.ndim - 1)))
    scaled = upstream * norm_gain
    raw_grad = inverse * (scaled - normed * jnp.mean(scaled * normed, axis=-1, keepdims=True))
    return (raw_grad, gain_part)


def open_pairs(windows, tile_size):
    span = 3 * tile_size
    spots = jnp.arange(span * span, dtype=jnp.int32)
    step_rows = spots // span // tile_size - 1
    step_cols = spots % span // tile_size - 1
    tile_row = lax.axis_index("ty") + step_rows
    tile_col = lax.axis_index("tx") + step_cols
    inside = (
        (tile_row >= 0)
        & (tile_row < lax.axis_size("ty"))
        & (tile_col >= 0)
        & (tile_col < lax.axis_size("tx"))
    )
    reach_rows = ((windows[:, 0] - 1) // 2)[:, None]
    reach_cols = ((windows[:, 1] - 1) // 2)[:, None]
    within = (jnp.abs(step_rows)[None, :] <= reach_rows) & (
        jnp.abs(step_cols)[None, :] <= reach_cols
    )
    return inside[None, :] & within


def gathered(cells, sides, width):
    for axis, dim in reversed(sides):
        count = lax.axis_size(axis)
        ends = count - 1
        full = cells.shape[dim]
        head = lax.slice_in_dim(cells, 0, width, axis=dim)
        middle = lax.slice_in_dim(cells, width, full - width, axis=dim).astype(jnp.float32)
        tail = lax.slice_in_dim(cells, full - width, full, axis=dim)
        from_right = lax.ppermute(head.astype(jnp.bfloat16), axis, [((i + 1) % count, i) for i in range(ends)])
        from_left = lax.ppermute(tail.astype(jnp.bfloat16), axis, [(i, (i + 1) % count) for i in range(ends)])
        cells = middle + from_right.astype(jnp.float32) + from_left.astype(jnp.float32)
    return cells


def raw_backward(upstream, normed, inverse, norm_gain):
    scaled = upstream * norm_gain
    return inverse * (scaled - normed * jnp.mean(scaled * normed, axis=-1, keepdims=True))


def query_side(queries, keys_near, values_near, grad_out, open_mask, score_scale):
    scores = product("qhc,mhc->hqm", queries, keys_near) * score_scale
    weights = jnp.where(open_mask[:, None, :], jnp.exp(scores), 0.0)
    totals = jnp.sum(weights, axis=2)
    shares = weights / totals[:, :, None]
    shares_low = shares.astype(jnp.bfloat16)
    output = product("hqm,mhc->qhc", shares_low, values_near).astype(jnp.bfloat16)
    output_back = lax.optimization_barrier(output).astype(jnp.float32)
    row_delta = jnp.sum(grad_out.astype(jnp.float32) * output_back, axis=-1)
    share_grad = product("qhc,mhc->hqm", grad_out, values_near)
    score_grad = (shares * (share_grad - row_delta.T[:, :, None])).astype(jnp.bfloat16)
    query_grad = product("hqm,mhc->qhc", score_grad, keys_near) * score_scale
    value_part = product("hqm,qhc->hmc", shares_low, grad_out)
    key_part = product("hqm,qhc->hmc", score_grad, queries) * score_scale
    return (output, query_grad, key_part, value_part)


def body(q_raw, k_raw, values, d_out, q_gain, k_gain, windows):
    head_count = windows.shape[0]
    share_len = q_gain.shape[0]
    head_size = share_len * lax.axis_size("fsdp")
    gain_slots = jnp.zeros((2, head_size), jnp.float32)
    gain_slots = lax.dynamic_update_slice_in_dim(
        gain_slots, jnp.stack([q_gain, k_gain]), lax.axis_index("fsdp") * share_len, 1
    )
    gains = xor_sum(gain_slots, "fsdp")
    q_gain_all, k_gain_all = gains[0], gains[1]
    frame_count, row_count, col_count, feature_count = q_raw.shape
    score_scale = 1.0 / math.sqrt(head_size)
    sides = (("ty", 2), ("tx", 3))
    arrived = padded(jnp.stack([k_raw, values]), sides, TILE)
    q_normed, q_inverse, q_hat = normalize(q_raw, q_gain_all, head_count)
    k_normed, k_inverse, _ = normalize(k_raw, k_gain_all, head_count)
    k_normed_near, _, k_hat_near = normalize(arrived[0], k_gain_all, head_count)
    open_mask = open_pairs(windows, TILE)
    local_rows = row_count * col_count
    near_rows = (row_count + 2 * TILE) * (col_count + 2 * TILE)

    def as_local(field):
        return field.reshape(frame_count, local_rows, head_count, head_size)

    def as_near(field):
        return field.reshape(frame_count, near_rows, head_count, head_size)

    def frame_query(queries, keys_near, values_near, grad_out):
        return query_side(queries, keys_near, values_near, grad_out, open_mask, score_scale)

    output, query_grad, key_part, value_part = jax.vmap(frame_query)(
        as_local(q_hat), as_near(k_hat_near), as_near(arrived[1]), as_local(d_out)
    )
    q_upstream = query_grad.reshape(q_normed.shape)
    q_part = jnp.sum(q_upstream * q_normed, axis=(0, 1, 2, 3))
    k_part = jnp.sum(key_part * jnp.swapaxes(as_near(k_normed_near), 1, 2), axis=(0, 1, 2))
    gain_parts = jnp.stack([q_part, k_part])
    plane_sum = xor_sum(xor_sum(gain_parts, "tx"), "ty")
    plane_sum, key_part, value_part = lax.optimization_barrier((plane_sum, key_part, value_part))
    owner_count = lax.axis_size("fsdp")
    pieces = plane_sum.reshape(2, owner_count, share_len).transpose(1, 0, 2)
    owned = lax.all_to_all(pieces, "fsdp", 0, 0, tiled=True).sum(axis=0)
    near_shape = (frame_count, head_count, row_count + 2 * TILE, col_count + 2 * TILE, head_size)

    def summed_of(part):
        cells = gathered(part.reshape(near_shape), sides, TILE)
        return cells.transpose(0, 2, 3, 1, 4)

    key_summed = summed_of(key_part)
    value_summed = summed_of(value_part)
    k_upstream = key_summed.reshape(k_normed.shape)
    q_field_grad = raw_backward(q_upstream, q_normed, q_inverse, q_gain_all)
    k_field_grad = raw_backward(k_upstream, k_normed, k_inverse, k_gain_all)
    return (
        output.reshape(q_raw.shape),
        q_field_grad.reshape(q_raw.shape).astype(jnp.bfloat16),
        k_field_grad.reshape(k_raw.shape).astype(jnp.bfloat16),
        value_summed.reshape(values.shape).astype(jnp.bfloat16),
        owned[0],
        owned[1],
    )


def solution(mesh):
    return jax.shard_map(
        body,
        mesh=mesh,
        in_specs=(
            P("fsdp", "ty", "tx", None),
            P("fsdp", "ty", "tx", None),
            P("fsdp", "ty", "tx", None),
            P("fsdp", "ty", "tx", None),
            P("fsdp"),
            P("fsdp"),
            P(),
        ),
        out_specs=(
            P("fsdp", "ty", "tx", None),
            P("fsdp", "ty", "tx", None),
            P("fsdp", "ty", "tx", None),
            P("fsdp", "ty", "tx", None),
            P("fsdp"),
            P("fsdp"),
        ),
        check_vma=False,
    )
```

profile of v0, /device:TPU:6, one launch (start us, length us, event | category | flops | bytes accessed | tf_op | source)
XLA Modules:
  0.0 342.9 jit_solution(17468888338691296430)
XLA Ops:
  14.2 6.7 %collective-permute-start.2 = (bf16[2,2,24,8,1536]{4,3,2,1,0:T(8,128)(2,1)}, bf16[2,2,24,8,1536]{4,3,2,1,0:T(8,128)(2,1)}, u32[]{:S(2)}, u32[]{:S(2)}) collective-permute-start(bf16[2,2,24,8,1536]{4,3,2,1,0:T(8,128)(2,1)} %pad_maximum_fusion.1), channel_id=1, source_target_pairs={{0,1},{1,2},{2,3},{3,4},{4,5},{5,6},{6,7},{8,9},{9,10},{10,11},{11... | collective-permute-start | bytes 7077896 | tf_op jit(solution)/shard_map/ppermute | solution.py:22
  21.1 3.9 %collective-permute-start.4 = (f32[2,128]{1,0:T(2,128)S(1)}, f32[2,128]{1,0:T(2,128)S(1)}, u32[]{:S(2)}, u32[]{:S(2)}) collective-permute-start(f32[2,128]{1,0:T(2,128)S(1)} %dynamic_update_slice.5), channel_id=1, source_target_pairs={{0,32},{32,0},{64,96},{96,64},{128,160},{160,128},{192,224},{224,1... | collective-permute-start | bytes 3080 | tf_op jit(solution)/shard_map/ppermute | solution.py:35
  26.7 5.4 %collective-permute-start.5 = (f32[2,128]{1,0:T(2,128)S(1)}, f32[2,128]{1,0:T(2,128)S(1)}, u32[]{:S(2)}, u32[]{:S(2)}) collective-permute-start(f32[2,128]{1,0:T(2,128)S(1)} %add.178), channel_id=1, source_target_pairs={{0,64},{32,96},{64,0},{96,32},{128,192},{160,224},{192,128},{224,1... | collective-permute-start | bytes 3080 | tf_op jit(solution)/shard_map/ppermute | solution.py:35
  33.6 9.1 %collective-permute-start.6 = (f32[2,128]{1,0:T(2,128)S(1)}, f32[2,128]{1,0:T(2,128)S(1)}, u32[]{:S(2)}, u32[]{:S(2)}) collective-permute-start(f32[2,128]{1,0:T(2,128)S(1)} %add.179), channel_id=1, source_target_pairs={{0,128},{32,160},{64,192},{96,224},{128,0},{160,32},{192,64},{224,... | collective-permute-start | bytes 3080 | tf_op jit(solution)/shard_map/ppermute | solution.py:35
  44.3 15.7 %collective-permute-start.7 = (f32[2,128]{1,0:T(2,128)S(1)}, f32[2,128]{1,0:T(2,128)S(1)}, u32[]{:S(2)}, u32[]{:S(2)}) collective-permute-start(f32[2,128]{1,0:T(2,128)S(1)} %add.180), channel_id=1, source_target_pairs={{0,256},{32,288},{64,320},{96,352},{128,384},{160,416},{192,448},{... | collective-permute-start | bytes 3080 | tf_op jit(solution)/shard_map/ppermute | solution.py:35
  62.1 24.2 %collective-permute-start.8 = (f32[2,128]{1,0:T(2,128)}, f32[2,128]{1,0:T(2,128)}, u32[]{:S(2)}, u32[]{:S(2)}) collective-permute-start(f32[2,128]{1,0:T(2,128)} %add.181), channel_id=1, source_target_pairs={{0,512},{32,544},{64,576},{96,608},{128,640},{160,672},{192,704},{... | collective-permute-start | bytes 3080 | tf_op jit(solution)/shard_map/ppermute | solution.py:35
  97.8 5.1 %slice_convert_fusion = (f32[1,2,24,24,1536]{4,3,2,1,0:T(8,128)}, bf16[1,2,24,24,1536]{4,3,2,1,0:T(8,128)(2,1)}) fusion(bf16[2,2,24,24,1536]{4,3,2,1,0:T(8,128)(2,1)S(1)} %pad_maximum_fusion), kind=kLoop, calls=%fused_computation.8 | loop fusion | flops 1769472 | bytes 17694720 | tf_op jit(solution)/shard_map/convert_element_type | solution.py:45
  102.9 9.1 %mul.198 = f32[2,24,24,12,128]{4,3,2,1,0:T(8,128)} reshape(f32[1,2,24,24,1536]{4,3,2,1,0:T(8,128)} %fusion.12) | data formatting | bytes 14155776 | tf_op jit(solution)/shard_map/mul | solution.py:47
  112.0 6.2 %reduce_sum.91 = f32[2,24,24,12]{3,2,1,0:T(8,128)S(1)} reduce(f32[2,24,24,12,128]{4,3,2,1,0:T(8,128)} %mul.198, f32[]{:T(128)} %constant.95.clone.1), dimensions={4}, to_apply=%region_1.0 | reduce | flops 1755648 | bytes 7133188 | tf_op jit(solution)/shard_map/reduce_sum | solution.py:47
  118.8 9.1 %reshape.201 = f32[2,576,12,128]{3,2,1,0:T(8,128)} reshape(f32[1,2,24,24,1536]{4,3,2,1,0:T(8,128)} %get-tuple-element.18) | data formatting | bytes 14155776 | tf_op jit(solution)/shard_map/convert_element_type | solution.py:45
  127.9 7.4 %reshape_squeeze.3 = bf16[2,576,12,128]{3,2,1,0:T(8,128)(2,1)} reshape(bf16[1,2,24,24,1536]{4,3,2,1,0:T(8,128)(2,1)} %get-tuple-element.19) | data formatting | bytes 7077888 | tf_op jit(solution)/shard_map/reshape;squeeze | solution.py:141
  135.3 8.1 %fusion.3 = (f32[2,12,64]{2,1,0:T(8,128)S(1)}, f32[2,12,64,576]{3,2,1,0:T(8,128)S(1)}) fusion(pred[12,576]{1,0:T(8,128)(4,1)S(1)} %copy-done.9, f32[2,576,12,128]{3,2,1,0:T(8,128)} %reshape.201, f32[128]{0:T(128)S(1)} %copy-done.11, f32[2,576,12]{1,2,0:T(8,128)S(1)} %reshape.204, f32[128]{0:T(128)S(1)} %copy-done.14, f32[2,64,12]{1,2,0:T(8,128)S(1)} %copy.59, ...), kind=kOutput, calls=%fused_computation.11 | convolution fusion | flops 235043328 | bytes 11478784 | tf_op jit(solution)/shard_map/vmap(qhc,mhc->hqm)/dot_general | solution.py:41
  149.9 7.5 %fusion = (f32[128]{0:T(128)S(1)}, f32[2,12,576,128]{3,2,1,0:T(8,128)}) fusion(f32[2,576,12,128]{3,2,1,0:T(8,128)S(1)} %bitcast.102, f32[2,576,12]{1,2,0:T(8,128)S(1)} %reshape.204, bf16[2,12,64,576]{3,2,1,0:T(8,128)(2,1)S(1)} %fusion.1, f32[128]{0:T(128)S(1)} %copy-done.14, f32[2,64,12]{1,2,0:T(8,128)S(1)} %copy.59, f32[2,64,12,128]{3,2,1,0:T(8,128)S(1)} %reshape.192), kind=kOutput, calls=%fused_computation.2 | convolution fusion | flops 234160000 | bytes 16774144 | tf_op jit(solution)/shard_map/vmap(hqm,qhc->hmc)/dot_general | solution.py:41
  157.4 5.8 %multiply_reduce_fusion.1 = (f32[128]{0:T(128)S(1)}, f32[2,64,12]{1,2,0:T(8,128)}, f32[2,12,128,64]{2,3,1,0:T(8,128)S(1)}) fusion(f32[2,64,12]{1,2,0:T(8,128)S(1)} %copy.59, f32[2,64,12,128]{3,2,1,0:T(8,128)S(1)} %reshape.192, f32[128]{0:T(128)S(1)} %copy-done.18, bf16[2,12,64,576]{3,2,1,0:T(8,128)(2,1)S(1)} %fusion.1, ...), kind=kOutput, calls=%fused_computation.47 | convolution fusion | flops 233175424 | bytes 10489344 | tf_op jit(solution)/shard_map/vmap(hqm,mhc->qhc)/dot_general | solution.py:41
  169.3 4.9 %collective-permute-start.10 = (f32[2,128]{1,0:T(2,128)S(1)}, f32[2,128]{1,0:T(2,128)S(1)}, u32[]{:S(2)}, u32[]{:S(2)}) collective-permute-start(f32[2,128]{1,0:T(2,128)S(1)} %fusion.54), channel_id=1, source_target_pairs={{0,2},{1,3},{2,0},{3,1},{4,6},{5,7},{6,4},{7,5},{8,10},{9,11},{10,... | collective-permute-start | bytes 3080 | tf_op jit(solution)/shard_map/ppermute | solution.py:35
  180.0 4.4 %collective-permute-done.11 = f32[2,128]{1,0:T(2,128)S(1)} collective-permute-done((f32[2,128]{1,0:T(2,128)S(1)}, f32[2,128]{1,0:T(2,128)S(1)}, u32[]{:S(2)}, u32[]{:S(2)}) %collective-permute-start.11) | collective-permute-done | bytes 1056 | tf_op jit(solution)/shard_map/ppermute | solution.py:35
  184.4 51.0 %collective-permute-start.12 = (f32[2,128]{1,0:T(2,128)S(1)}, f32[2,128]{1,0:T(2,128)S(1)}, u32[]{:S(2)}, u32[]{:S(2)}) collective-permute-start(f32[2,128]{1,0:T(2,128)S(1)} %add.188), channel_id=1, source_target_pairs={{0,8},{8,0},{16,24},{24,16},{1,9},{9,1},{17,25},{25,17},{2,10},{10... | collective-permute-start | bytes 3080 | tf_op jit(solution)/shard_map/ppermute | solution.py:35
  235.4 6.7 %fusion.19 = f32[2,12,576,128]{3,2,1,0:T(8,128)} fusion(bf16[2,64,12,128]{3,2,1,0:T(8,128)(2,1)S(1)} %reshape.194, f32[2,12,64,576]{3,2,1,0:T(8,128)} %copy-done.2, f32[2,12,64]{2,1,0:T(8,128)} %copy-done.15, pred[12,576]{1,0:T(8,128)(4,1)} %and_and_fusion), kind=kOutput, calls=%fused_computation.26 | convolution fusion | flops 230031360 | bytes 11023104 | tf_op jit(solution)/shard_map/vmap(hqm,qhc->hmc)/dot_general | solution.py:41
  242.1 12.9 %collective-permute-start.13 = (f32[2,128]{1,0:T(2,128)S(1)}, f32[2,128]{1,0:T(2,128)S(1)}, u32[]{:S(2)}, u32[]{:S(2)}) collective-permute-start(f32[2,128]{1,0:T(2,128)S(1)} %add.189), channel_id=1, source_target_pairs={{0,16},{8,24},{16,0},{24,8},{1,17},{9,25},{17,1},{25,9},{2,18},{10... | collective-permute-start | bytes 3080 | tf_op jit(solution)/shard_map/ppermute | solution.py:35
  265.6 6.1 %collective-permute-start.15 = (bf16[2,12,24,8,128]{4,3,2,1,0:T(8,128)(2,1)}, bf16[2,12,24,8,128]{4,3,2,1,0:T(8,128)(2,1)}, u32[]{:S(2)}, u32[]{:S(2)}) collective-permute-start(bf16[2,12,24,8,128]{4,3,2,1,0:T(8,128)(2,1)} %get-tuple-element.23), channel_id=1, source_target_pairs={{0,1},{1,2},{2,3},{3,4},{4,5},{5,6},{6,7},{8,9},{9,10},{10,11},{11... | collective-permute-start | bytes 3538952 | tf_op jit(solution)/shard_map/ppermute | solution.py:89
  284.7 7.8 %collective-permute-start.19 = (bf16[2,12,24,8,128]{4,3,2,1,0:T(8,128)(2,1)}, bf16[2,12,24,8,128]{4,3,2,1,0:T(8,128)(2,1)}, u32[]{:S(2)}, u32[]{:S(2)}) collective-permute-start(bf16[2,12,24,8,128]{4,3,2,1,0:T(8,128)(2,1)} %get-tuple-element.21), channel_id=1, source_target_pairs={{0,1},{1,2},{2,3},{3,4},{4,5},{5,6},{6,7},{8,9},{9,10},{10,11},{11... | collective-permute-start | bytes 3538952 | tf_op jit(solution)/shard_map/ppermute | solution.py:89
  295.0 5.2 %all-to-all-done = f32[32,2,4]{2,1,0:T(2,128)S(1)} async-done(((f32[32,2,4]{2,1,0:T(2,128)}), f32[32,2,4]{2,1,0:T(2,128)S(1)}, u32[]{:S(2)}, u32[]{:S(2)}) %all-to-all-start) | async-done | bytes 1056 | tf_op jit(solution)/shard_map/all_to_all | solution.py:157
  308.2 12.8 %collective-permute-done.18 = bf16[2,12,24,8,128]{4,3,2,1,0:T(8,128)(2,1)} collective-permute-done((bf16[2,12,24,8,128]{4,3,2,1,0:T(8,128)(2,1)}, bf16[2,12,24,8,128]{4,3,2,1,0:T(8,128)(2,1)}, u32[]{:S(2)}, u32[]{:S(2)}) %collective-permute-start.18) | collective-permute-done | bytes 1179680 | tf_op jit(solution)/shard_map/ppermute | solution.py:88
  322.1 4.4 %fusion.60 = (bf16[2,12,24,8,128]{4,3,2,1,0:T(8,128)(2,1)S(1)}, f32[2,12,24,8,128]{4,3,2,1,0:T(8,128)}) fusion(bf16[2,12,24,8,128]{4,3,2,1,0:T(8,128)(2,1)} %collective-permute-done.19, bf16[2,12,24,8,128]{4,3,2,1,0:T(8,128)(2,1)} %collective-permute-done.18, f32[2,12,24,24,128]{4,3,2,1,0:T(8,128)} %bitcast.109), kind=kLoop, calls=%fused_computation.119 | loop fusion | flops 2949120 | bytes 8257536 | tf_op jit(solution)/shard_map/convert.3
  (152 shorter events, 102.1 us)
Async XLA Ops:
  1.9 88.5 %copy-start = (bf16[2,8,8,1536]{3,2,1,0:T(8,128)(2,1)S(1)}, bf16[2,8,8,1536]{3,2,1,0:T(8,128)(2,1)}, u32[]{:S(2)}) copy-start(bf16[2,8,8,1536]{3,2,1,0:T(8,128)(2,1)} %param.8) | copy-start | bytes 1179652
  1.9 4.5 %collective-permute-start.1 = (bf16[2,2,8,8,1536]{4,3,2,1,0:T(8,128)(2,1)S(1)}, bf16[2,2,8,8,1536]{4,3,2,1,0:T(8,128)(2,1)S(1)}, u32[]{:S(2)}, u32[]{:S(2)}) collective-permute-start(bf16[2,2,8,8,1536]{4,3,2,1,0:T(8,128)(2,1)S(1)} %pad_maximum_fusion.2), channel_id=1, source_target_pairs={{8,0},{16,8},{24,16},{9,1},{17,9},{25,17},{10,2},{18,10},{26,18},{... | collective-permute-start | bytes 2359304 | tf_op jit(solution)/shard_map/ppermute | solution.py:24
  3.4 4.9 %collective-permute-start = (bf16[2,2,8,8,1536]{4,3,2,1,0:T(8,128)(2,1)S(1)}, bf16[2,2,8,8,1536]{4,3,2,1,0:T(8,128)(2,1)S(1)}, u32[]{:S(2)}, u32[]{:S(2)}) collective-permute-start(bf16[2,2,8,8,1536]{4,3,2,1,0:T(8,128)(2,1)S(1)} %pad_maximum_fusion.2), channel_id=1, source_target_pairs={{0,8},{8,16},{16,24},{1,9},{9,17},{17,25},{2,10},{10,18},{18,26},{... | collective-permute-start | bytes 2359304 | tf_op jit(solution)/shard_map/ppermute | solution.py:22
  11.4 79.0 %collective-permute-start.3 = (bf16[2,2,24,8,1536]{4,3,2,1,0:T(8,128)(2,1)}, bf16[2,2,24,8,1536]{4,3,2,1,0:T(8,128)(2,1)}, u32[]{:S(2)}, u32[]{:S(2)}) collective-permute-start(bf16[2,2,24,8,1536]{4,3,2,1,0:T(8,128)(2,1)} %pad_maximum_fusion.1), channel_id=1, source_target_pairs={{1,0},{2,1},{3,2},{4,3},{5,4},{6,5},{7,6},{9,8},{10,9},{11,10},{12... | collective-permute-start | bytes 7077896 | tf_op jit(solution)/shard_map/ppermute | solution.py:24
  14.2 76.3 %collective-permute-start.2 = (bf16[2,2,24,8,1536]{4,3,2,1,0:T(8,128)(2,1)}, bf16[2,2,24,8,1536]{4,3,2,1,0:T(8,128)(2,1)}, u32[]{:S(2)}, u32[]{:S(2)}) collective-permute-start(bf16[2,2,24,8,1536]{4,3,2,1,0:T(8,128)(2,1)} %pad_maximum_fusion.1), channel_id=1, source_target_pairs={{0,1},{1,2},{2,3},{3,4},{4,5},{5,6},{6,7},{8,9},{9,10},{10,11},{11... | collective-permute-start | bytes 7077896 | tf_op jit(solution)/shard_map/ppermute | solution.py:22
  21.1 5.5 %collective-permute-start.4 = (f32[2,128]{1,0:T(2,128)S(1)}, f32[2,128]{1,0:T(2,128)S(1)}, u32[]{:S(2)}, u32[]{:S(2)}) collective-permute-start(f32[2,128]{1,0:T(2,128)S(1)} %dynamic_update_slice.5), channel_id=1, source_target_pairs={{0,32},{32,0},{64,96},{96,64},{128,160},{160,128},{192,224},{224,1... | collective-permute-start | bytes 3080 | tf_op jit(solution)/shard_map/ppermute | solution.py:35
  26.7 6.9 %collective-permute-start.5 = (f32[2,128]{1,0:T(2,128)S(1)}, f32[2,128]{1,0:T(2,128)S(1)}, u32[]{:S(2)}, u32[]{:S(2)}) collective-permute-start(f32[2,128]{1,0:T(2,128)S(1)} %add.178), channel_id=1, source_target_pairs={{0,64},{32,96},{64,0},{96,32},{128,192},{160,224},{192,128},{224,1... | collective-permute-start | bytes 3080 | tf_op jit(solution)/shard_map/ppermute | solution.py:35
  33.6 10.6 %collective-permute-start.6 = (f32[2,128]{1,0:T(2,128)S(1)}, f32[2,128]{1,0:T(2,128)S(1)}, u32[]{:S(2)}, u32[]{:S(2)}) collective-permute-start(f32[2,128]{1,0:T(2,128)S(1)} %add.179), channel_id=1, source_target_pairs={{0,128},{32,160},{64,192},{96,224},{128,0},{160,32},{192,64},{224,... | collective-permute-start | bytes 3080 | tf_op jit(solution)/shard_map/ppermute | solution.py:35
  44.3 17.3 %collective-permute-start.7 = (f32[2,128]{1,0:T(2,128)S(1)}, f32[2,128]{1,0:T(2,128)S(1)}, u32[]{:S(2)}, u32[]{:S(2)}) collective-permute-start(f32[2,128]{1,0:T(2,128)S(1)} %add.180), channel_id=1, source_target_pairs={{0,256},{32,288},{64,320},{96,352},{128,384},{160,416},{192,448},{... | collective-permute-start | bytes 3080 | tf_op jit(solution)/shard_map/ppermute | solution.py:35
  62.1 26.6 %collective-permute-start.8 = (f32[2,128]{1,0:T(2,128)}, f32[2,128]{1,0:T(2,128)}, u32[]{:S(2)}, u32[]{:S(2)}) collective-permute-start(f32[2,128]{1,0:T(2,128)} %add.181), channel_id=1, source_target_pairs={{0,512},{32,544},{64,576},{96,608},{128,640},{160,672},{192,704},{... | collective-permute-start | bytes 3080 | tf_op jit(solution)/shard_map/ppermute | solution.py:35
  163.2 5.5 %collective-permute-start.9 = (f32[2,128]{1,0:T(2,128)S(1)}, f32[2,128]{1,0:T(2,128)S(1)}, u32[]{:S(2)}, u32[]{:S(2)}) collective-permute-start(f32[2,128]{1,0:T(2,128)S(1)} %pad_maximum_fusion.4), channel_id=1, source_target_pairs={{0,1},{1,0},{2,3},{3,2},{4,5},{5,4},{6,7},{7,6},{8,9},{9,8},{10,11... | collective-permute-start | bytes 3080 | tf_op jit(solution)/shard_map/ppermute | solution.py:35
  169.3 7.4 %collective-permute-start.10 = (f32[2,128]{1,0:T(2,128)S(1)}, f32[2,128]{1,0:T(2,128)S(1)}, u32[]{:S(2)}, u32[]{:S(2)}) collective-permute-start(f32[2,128]{1,0:T(2,128)S(1)} %fusion.54), channel_id=1, source_target_pairs={{0,2},{1,3},{2,0},{3,1},{4,6},{5,7},{6,4},{7,5},{8,10},{9,11},{10,... | collective-permute-start | bytes 3080 | tf_op jit(solution)/shard_map/ppermute | solution.py:35
  177.4 7.0 %collective-permute-start.11 = (f32[2,128]{1,0:T(2,128)S(1)}, f32[2,128]{1,0:T(2,128)S(1)}, u32[]{:S(2)}, u32[]{:S(2)}) collective-permute-start(f32[2,128]{1,0:T(2,128)S(1)} %fusion.70), channel_id=1, source_target_pairs={{0,4},{1,5},{2,6},{3,7},{4,0},{5,1},{6,2},{7,3},{8,12},{9,13},{10,... | collective-permute-start | bytes 3080 | tf_op jit(solution)/shard_map/ppermute | solution.py:35
  184.4 57.7 %collective-permute-start.12 = (f32[2,128]{1,0:T(2,128)S(1)}, f32[2,128]{1,0:T(2,128)S(1)}, u32[]{:S(2)}, u32[]{:S(2)}) collective-permute-start(f32[2,128]{1,0:T(2,128)S(1)} %add.188), channel_id=1, source_target_pairs={{0,8},{8,0},{16,24},{24,16},{1,9},{9,1},{17,25},{25,17},{2,10},{10... | collective-permute-start | bytes 3080 | tf_op jit(solution)/shard_map/ppermute | solution.py:35
  242.1 14.4 %collective-permute-start.13 = (f32[2,128]{1,0:T(2,128)S(1)}, f32[2,128]{1,0:T(2,128)S(1)}, u32[]{:S(2)}, u32[]{:S(2)}) collective-permute-start(f32[2,128]{1,0:T(2,128)S(1)} %add.189), channel_id=1, source_target_pairs={{0,16},{8,24},{16,0},{24,8},{1,17},{9,25},{17,1},{25,9},{2,18},{10... | collective-permute-start | bytes 3080 | tf_op jit(solution)/shard_map/ppermute | solution.py:35
  262.3 38.4 %collective-permute-start.14 = (bf16[2,12,24,8,128]{4,3,2,1,0:T(8,128)(2,1)}, bf16[2,12,24,8,128]{4,3,2,1,0:T(8,128)(2,1)}, u32[]{:S(2)}, u32[]{:S(2)}) collective-permute-start(bf16[2,12,24,8,128]{4,3,2,1,0:T(8,128)(2,1)} %get-tuple-element.22), channel_id=1, source_target_pairs={{1,0},{2,1},{3,2},{4,3},{5,4},{6,5},{7,6},{9,8},{10,9},{11,10},{12... | collective-permute-start | bytes 3538952 | tf_op jit(solution)/shard_map/ppermute | solution.py:88
  265.6 35.1 %collective-permute-start.15 = (bf16[2,12,24,8,128]{4,3,2,1,0:T(8,128)(2,1)}, bf16[2,12,24,8,128]{4,3,2,1,0:T(8,128)(2,1)}, u32[]{:S(2)}, u32[]{:S(2)}) collective-permute-start(bf16[2,12,24,8,128]{4,3,2,1,0:T(8,128)(2,1)} %get-tuple-element.23), channel_id=1, source_target_pairs={{0,1},{1,2},{2,3},{3,4},{4,5},{5,6},{6,7},{8,9},{9,10},{10,11},{11... | collective-permute-start | bytes 3538952 | tf_op jit(solution)/shard_map/ppermute | solution.py:89
  273.2 27.0 %all-to-all-start = ((f32[32,2,4]{2,1,0:T(2,128)}), f32[32,2,4]{2,1,0:T(2,128)S(1)}, u32[]{:S(2)}, u32[]{:S(2)}) async-start(f32[32,2,4]{2,1,0:T(2,128)} %copy.82), calls=%async_computation | async-start | bytes 65536 | tf_op jit(solution)/shard_map/all_to_all | solution.py:157
  282.8 38.2 %collective-permute-start.18 = (bf16[2,12,24,8,128]{4,3,2,1,0:T(8,128)(2,1)}, bf16[2,12,24,8,128]{4,3,2,1,0:T(8,128)(2,1)}, u32[]{:S(2)}, u32[]{:S(2)}) collective-permute-start(bf16[2,12,24,8,128]{4,3,2,1,0:T(8,128)(2,1)} %get-tuple-element.20), channel_id=1, source_target_pairs={{1,0},{2,1},{3,2},{4,3},{5,4},{6,5},{7,6},{9,8},{10,9},{11,10},{12... | collective-permute-start | bytes 3538952 | tf_op jit(solution)/shard_map/ppermute | solution.py:88
  284.7 37.4 %collective-permute-start.19 = (bf16[2,12,24,8,128]{4,3,2,1,0:T(8,128)(2,1)}, bf16[2,12,24,8,128]{4,3,2,1,0:T(8,128)(2,1)}, u32[]{:S(2)}, u32[]{:S(2)}) collective-permute-start(bf16[2,12,24,8,128]{4,3,2,1,0:T(8,128)(2,1)} %get-tuple-element.21), channel_id=1, source_target_pairs={{0,1},{1,2},{2,3},{3,4},{4,5},{5,6},{6,7},{8,9},{9,10},{10,11},{11... | collective-permute-start | bytes 3538952 | tf_op jit(solution)/shard_map/ppermute | solution.py:89
  303.7 28.9 %collective-permute-start.16 = (bf16[2,12,8,8,128]{4,3,2,1,0:T(8,128)(2,1)S(1)}, bf16[2,12,8,8,128]{4,3,2,1,0:T(8,128)(2,1)S(1)}, u32[]{:S(2)}, u32[]{:S(2)}) collective-permute-start(bf16[2,12,8,8,128]{4,3,2,1,0:T(8,128)(2,1)S(1)} %get-tuple-element.26), channel_id=1, source_target_pairs={{8,0},{16,8},{24,16},{9,1},{17,9},{25,17},{10,2},{18,10},{26,18},{... | collective-permute-start | bytes 1179656 | tf_op jit(solution)/shard_map/ppermute | solution.py:88
  305.0 27.6 %collective-permute-start.17 = (bf16[2,12,8,8,128]{4,3,2,1,0:T(8,128)(2,1)S(1)}, bf16[2,12,8,8,128]{4,3,2,1,0:T(8,128)(2,1)S(1)}, u32[]{:S(2)}, u32[]{:S(2)}) collective-permute-start(bf16[2,12,8,8,128]{4,3,2,1,0:T(8,128)(2,1)S(1)} %get-tuple-element.27), channel_id=1, source_target_pairs={{0,8},{8,16},{16,24},{1,9},{9,17},{17,25},{2,10},{10,18},{18,26},{... | collective-permute-start | bytes 1179656 | tf_op jit(solution)/shard_map/ppermute | solution.py:89
  327.5 13.2 %collective-permute-start.20 = (bf16[2,12,8,8,128]{4,3,2,1,0:T(8,128)(2,1)}, bf16[2,12,8,8,128]{4,3,2,1,0:T(8,128)(2,1)}, u32[]{:S(2)}, u32[]{:S(2)}) collective-permute-start(bf16[2,12,8,8,128]{4,3,2,1,0:T(8,128)(2,1)} %get-tuple-element.24), channel_id=1, source_target_pairs={{8,0},{16,8},{24,16},{9,1},{17,9},{25,17},{10,2},{18,10},{26,18},{... | collective-permute-start | bytes 1179656 | tf_op jit(solution)/shard_map/ppermute | solution.py:88
  328.8 11.9 %collective-permute-start.21 = (bf16[2,12,8,8,128]{4,3,2,1,0:T(8,128)(2,1)}, bf16[2,12,8,8,128]{4,3,2,1,0:T(8,128)(2,1)}, u32[]{:S(2)}, u32[]{:S(2)}) collective-permute-start(bf16[2,12,8,8,128]{4,3,2,1,0:T(8,128)(2,1)} %get-tuple-element.25), channel_id=1, source_target_pairs={{0,8},{8,16},{16,24},{1,9},{9,17},{17,25},{2,10},{10,18},{18,26},{... | collective-permute-start | bytes 1179656 | tf_op jit(solution)/shard_map/ppermute | solution.py:89
  (24 other events, 499.9 us)
where the time goes:
time: 349 us; the launch traced here: 343 us
  starting transfers between devices  177 us (51%)
  other arithmetic  51.5 us (15%)
  local copies, waits for them, and re-layouts  44.3 us (13%)
  waiting for transfers between devices  34.8 us (10%)
  matrix products  33.6 us (10%)
    ppermute x10, starting transfers between devices, xor_sum(): lax.ppermute(cells, axis, [(i, i ^ step) for i in range(count)])  131 us
    dot_general x6, matrix products, product(): return jnp.einsum(form, left, right, preferred_element_type=jnp.float32)  33.6 us
    ppermute x4, starting transfers between devices, gathered(): lax.ppermute(tail.astype(jnp.bfloat16), axis, [(i, (i + 1) % count) for i...  20.9 us
    another operation x4, other arithmetic  14.5 us
    ppermute x10, waiting for transfers between devices, xor_sum(): lax.ppermute(cells, axis, [(i, i ^ step) for i in range(count)])  13.8 us
    ppermute x4, waiting for transfers between devices, gathered(): lax.ppermute(head.astype(jnp.bfloat16), axis, [((i + 1) % count, i) for i...  12.8 us
    ppermute x2, starting transfers between devices, padded(): lax.ppermute(tail, axis, [(i, (i + 1) % count) for i in range(ends)])  9.8 us
    convert_element_type x1, local copies, waits for them, and re-layouts, normalize(): floats = raw_field.astype(jnp.float32)  9.12 us
  transfers between devices with their start and end apart: 23, of which 11 were waited for; matrix products, arithmetic and copies ran while one was open for 13% of the time, Pallas kernels for 0%

commit v1 on v0

--- a/solution.py
+++ b/solution.py
@@ -125,7 +125,7 @@
     q_gain_all, k_gain_all = gains[0], gains[1]
     frame_count, row_count, col_count, feature_count = q_raw.shape
     score_scale = 1.0 / math.sqrt(head_size)
-    sides = (("ty", 2), ("tx", 3))
+    sides = (("tx", 3), ("ty", 2))
     arrived = padded(jnp.stack([k_raw, values]), sides, TILE)
     q_normed, q_inverse, q_hat = normalize(q_raw, q_gain_all, head_count)
     k_normed, k_inverse, _ = normalize(k_raw, k_gain_all, head_count)

time: 349 us -> 315 us (0.903)
  starting transfers between devices: 177 us -> 141 us
  waiting for transfers between devices: 34.8 us -> 40 us
    ppermute x10, starting transfers between devices: 131 us -> 73.1 us  [xor_sum(): lax.ppermute(cells, axis, [(i, i ^ step) for i in range(count)])]
    all_to_all x1, starting transfers between devices: 3.85 us -> 21.5 us  [body(): owned = lax.all_to_all(pieces, 'fsdp', 0, 0, tiled=True).sum(axis=0)]
    ppermute x2, waiting for transfers between devices: 0.01 us -> 15.3 us  [padded(): lax.ppermute(head, axis, [((i + 1) % count, i) for i in range(ends)])]
    ppermute x4, waiting for transfers between devices: 12.8 us -> 0.01 us  [gathered(): lax.ppermute(head.astype(jnp.bfloat16), axis, [((i + 1) % count, i) for i...]
    all_to_all x1, waiting for transfers between devices: 5.18 us -> 10.2 us  [body(): owned = lax.all_to_all(pieces, 'fsdp', 0, 0, tiled=True).sum(axis=0)]
  transfers between devices with their start and end apart: 23 -> 23, of which waited for: 11 -> 11; matrix products, arithmetic and copies ran while one was open for 13% -> 14% of each run, Pallas kernels for 0% -> 0%
where the time goes in v1:
time: 315 us; the launch traced here: 311 us
  starting transfers between devices  141 us (45%)
  other arithmetic  51.6 us (16%)
  local copies, waits for them, and re-layouts  44.1 us (14%)
  waiting for transfers between devices  40 us (13%)
  matrix products  33.6 us (11%)
    ppermute x10, starting transfers between devices, xor_sum(): lax.ppermute(cells, axis, [(i, i ^ step) for i in range(count)])  73.1 us
    dot_general x6, matrix products, product(): return jnp.einsum(form, left, right, preferred_element_type=jnp.float32)  33.6 us
    ppermute x4, starting transfers between devices, gathered(): lax.ppermute(tail.astype(jnp.bfloat16), axis, [(i, (i + 1) % count) for i...  23 us
    all_to_all x1, starting transfers between devices, body(): owned = lax.all_to_all(pieces, 'fsdp', 0, 0, tiled=True).sum(axis=0)  21.5 us
    ppermute x2, waiting for transfers between devices, padded(): lax.ppermute(head, axis, [((i + 1) % count, i) for i in range(ends)])  15.3 us
    another operation x4, other arithmetic  14.6 us
    ppermute x10, waiting for transfers between devices, xor_sum(): lax.ppermute(cells, axis, [(i, i ^ step) for i in range(count)])  13.3 us
    ppermute x2, starting transfers between devices, padded(): lax.ppermute(tail, axis, [(i, (i + 1) % count) for i in range(ends)])  11.2 us
  transfers between devices with their start and end apart: 23, of which 11 were waited for; matrix products, arithmetic and copies ran while one was open for 14% of the time, Pallas kernels for 0%

profile of v1, /device:TPU:6, one launch (start us, length us, event | category | flops | bytes accessed | tf_op | source)
XLA Modules:
  0.0 311.4 jit_solution(163408161125298297)
XLA Ops:
  4.8 6.7 %collective-permute-start = (bf16[2,2,8,8,1536]{4,3,2,1,0:T(8,128)(2,1)S(1)}, bf16[2,2,8,8,1536]{4,3,2,1,0:T(8,128)(2,1)S(1)}, u32[]{:S(2)}, u32[]{:S(2)}) collective-permute-start(bf16[2,2,8,8,1536]{4,3,2,1,0:T(8,128)(2,1)S(1)} %pad_maximum_fusion.2), channel_id=1, source_target_pairs={{0,1},{1,2},{2,3},{3,4},{4,5},{5,6},{6,7},{8,9},{9,10},{10,11},{11... | collective-permute-start | bytes 2359304 | tf_op jit(solution)/shard_map/ppermute | solution.py:22
  11.5 15.3 %collective-permute-done.1 = bf16[2,2,8,8,1536]{4,3,2,1,0:T(8,128)(2,1)S(1)} collective-permute-done((bf16[2,2,8,8,1536]{4,3,2,1,0:T(8,128)(2,1)S(1)}, bf16[2,2,8,8,1536]{4,3,2,1,0:T(8,128)(2,1)S(1)}, u32[]{:S(2)}, u32[]{:S(2)}) %collective-permute-start.1) | collective-permute-done | bytes 786464 | tf_op jit(solution)/shard_map/ppermute | solution.py:24
  32.4 4.5 %collective-permute-start.2 = (bf16[2,2,8,24,1536]{4,3,2,1,0:T(8,128)(2,1)}, bf16[2,2,8,24,1536]{4,3,2,1,0:T(8,128)(2,1)}, u32[]{:S(2)}, u32[]{:S(2)}) collective-permute-start(bf16[2,2,8,24,1536]{4,3,2,1,0:T(8,128)(2,1)} %pad_maximum_fusion.1), channel_id=1, source_target_pairs={{0,8},{8,16},{16,24},{1,9},{9,17},{17,25},{2,10},{10,18},{18,26},{... | collective-permute-start | bytes 7077896 | tf_op jit(solution)/shard_map/ppermute | solution.py:22
  42.7 5.4 %collective-permute-start.5 = (f32[2,128]{1,0:T(2,128)S(1)}, f32[2,128]{1,0:T(2,128)S(1)}, u32[]{:S(2)}, u32[]{:S(2)}) collective-permute-start(f32[2,128]{1,0:T(2,128)S(1)} %add.178), channel_id=1, source_target_pairs={{0,64},{32,96},{64,0},{96,32},{128,192},{160,224},{192,128},{224,1... | collective-permute-start | bytes 3080 | tf_op jit(solution)/shard_map/ppermute | solution.py:35
  49.6 9.1 %collective-permute-start.6 = (f32[2,128]{1,0:T(2,128)S(1)}, f32[2,128]{1,0:T(2,128)S(1)}, u32[]{:S(2)}, u32[]{:S(2)}) collective-permute-start(f32[2,128]{1,0:T(2,128)S(1)} %add.179), channel_id=1, source_target_pairs={{0,128},{32,160},{64,192},{96,224},{128,0},{160,32},{192,64},{224,... | collective-permute-start | bytes 3080 | tf_op jit(solution)/shard_map/ppermute | solution.py:35
  60.2 15.7 %collective-permute-start.7 = (f32[2,128]{1,0:T(2,128)S(1)}, f32[2,128]{1,0:T(2,128)S(1)}, u32[]{:S(2)}, u32[]{:S(2)}) collective-permute-start(f32[2,128]{1,0:T(2,128)S(1)} %add.180), channel_id=1, source_target_pairs={{0,256},{32,288},{64,320},{96,352},{128,384},{160,416},{192,448},{... | collective-permute-start | bytes 3080 | tf_op jit(solution)/shard_map/ppermute | solution.py:35
  78.1 24.2 %collective-permute-start.8 = (f32[2,128]{1,0:T(2,128)}, f32[2,128]{1,0:T(2,128)}, u32[]{:S(2)}, u32[]{:S(2)}) collective-permute-start(f32[2,128]{1,0:T(2,128)} %add.181), channel_id=1, source_target_pairs={{0,512},{32,544},{64,576},{96,608},{128,640},{160,672},{192,704},{... | collective-permute-start | bytes 3080 | tf_op jit(solution)/shard_map/ppermute | solution.py:35
  113.7 5.1 %slice_convert_fusion = (f32[1,2,24,24,1536]{4,3,2,1,0:T(8,128)}, bf16[1,2,24,24,1536]{4,3,2,1,0:T(8,128)(2,1)}) fusion(bf16[2,2,24,24,1536]{4,3,2,1,0:T(8,128)(2,1)S(1)} %pad_maximum_fusion), kind=kLoop, calls=%fused_computation.8 | loop fusion | flops 1769472 | bytes 17694720 | tf_op jit(solution)/shard_map/convert_element_type | solution.py:45
  118.8 9.1 %mul.198 = f32[2,24,24,12,128]{4,3,2,1,0:T(8,128)} reshape(f32[1,2,24,24,1536]{4,3,2,1,0:T(8,128)} %fusion.12) | data formatting | bytes 14155776 | tf_op jit(solution)/shard_map/mul | solution.py:47
  127.9 6.2 %reduce_sum.91 = f32[2,24,24,12]{3,2,1,0:T(8,128)S(1)} reduce(f32[2,24,24,12,128]{4,3,2,1,0:T(8,128)} %mul.198, f32[]{:T(128)} %constant.95.clone.1), dimensions={4}, to_apply=%region_1.0 | reduce | flops 1755648 | bytes 7133188 | tf_op jit(solution)/shard_map/reduce_sum | solution.py:47
  134.7 9.1 %reshape.201 = f32[2,576,12,128]{3,2,1,0:T(8,128)} reshape(f32[1,2,24,24,1536]{4,3,2,1,0:T(8,128)} %get-tuple-element.18) | data formatting | bytes 14155776 | tf_op jit(solution)/shard_map/convert_element_type | solution.py:45
  143.8 7.4 %reshape_squeeze.3 = bf16[2,576,12,128]{3,2,1,0:T(8,128)(2,1)} reshape(bf16[1,2,24,24,1536]{4,3,2,1,0:T(8,128)(2,1)} %get-tuple-element.19) | data formatting | bytes 7077888 | tf_op jit(solution)/shard_map/reshape;squeeze | solution.py:141
  151.2 8.1 %fusion.3 = (f32[2,12,64]{2,1,0:T(8,128)S(1)}, f32[2,12,64,576]{3,2,1,0:T(8,128)S(1)}) fusion(pred[12,576]{1,0:T(8,128)(4,1)S(1)} %copy-done.9, f32[2,576,12,128]{3,2,1,0:T(8,128)} %reshape.201, f32[128]{0:T(128)S(1)} %copy-done.11, f32[2,576,12]{1,2,0:T(8,128)S(1)} %reshape.204, f32[128]{0:T(128)S(1)} %copy-done.14, f32[2,64,12]{1,2,0:T(8,128)S(1)} %copy.59, ...), kind=kOutput, calls=%fused_computation.11 | convolution fusion | flops 235043328 | bytes 11478784 | tf_op jit(solution)/shard_map/vmap(qhc,mhc->hqm)/dot_general | solution.py:41
  165.8 7.5 %fusion = (f32[128]{0:T(128)S(1)}, f32[2,12,576,128]{3,2,1,0:T(8,128)}) fusion(f32[2,576,12,128]{3,2,1,0:T(8,128)S(1)} %bitcast.102, f32[2,576,12]{1,2,0:T(8,128)S(1)} %reshape.204, bf16[2,12,64,576]{3,2,1,0:T(8,128)(2,1)S(1)} %fusion.1, f32[128]{0:T(128)S(1)} %copy-done.14, f32[2,64,12]{1,2,0:T(8,128)S(1)} %copy.59, f32[2,64,12,128]{3,2,1,0:T(8,128)S(1)} %reshape.192), kind=kOutput, calls=%fused_computation.2 | convolution fusion | flops 234160000 | bytes 16774144 | tf_op jit(solution)/shard_map/vmap(hqm,qhc->hmc)/dot_general | solution.py:41
  173.3 5.8 %multiply_reduce_fusion.1 = (f32[128]{0:T(128)S(1)}, f32[2,64,12]{1,2,0:T(8,128)}, f32[2,12,128,64]{2,3,1,0:T(8,128)S(1)}) fusion(f32[2,64,12]{1,2,0:T(8,128)S(1)} %copy.59, f32[2,64,12,128]{3,2,1,0:T(8,128)S(1)} %reshape.192, f32[128]{0:T(128)S(1)} %copy-done.18, bf16[2,12,64,576]{3,2,1,0:T(8,128)(2,1)S(1)} %fusion.1, ...), kind=kOutput, calls=%fused_computation.47 | convolution fusion | flops 233175424 | bytes 10489344 | tf_op jit(solution)/shard_map/vmap(hqm,mhc->qhc)/dot_general | solution.py:41
  193.0 5.5 %collective-permute-start.11 = (f32[2,128]{1,0:T(2,128)S(1)}, f32[2,128]{1,0:T(2,128)S(1)}, u32[]{:S(2)}, u32[]{:S(2)}) collective-permute-start(f32[2,128]{1,0:T(2,128)S(1)} %fusion.70), channel_id=1, source_target_pairs={{0,4},{1,5},{2,6},{3,7},{4,0},{5,1},{6,2},{7,3},{8,12},{9,13},{10,... | collective-permute-start | bytes 3080 | tf_op jit(solution)/shard_map/ppermute | solution.py:35
  202.0 6.7 %fusion.19 = f32[2,12,576,128]{3,2,1,0:T(8,128)} fusion(bf16[2,64,12,128]{3,2,1,0:T(8,128)(2,1)S(1)} %reshape.194, f32[2,12,64,576]{3,2,1,0:T(8,128)} %copy-done.2, f32[2,12,64]{2,1,0:T(8,128)} %copy-done.15, pred[12,576]{1,0:T(8,128)(4,1)} %and_and_fusion), kind=kOutput, calls=%fused_computation.26 | convolution fusion | flops 230031360 | bytes 11023104 | tf_op jit(solution)/shard_map/vmap(hqm,qhc->hmc)/dot_general | solution.py:41
  220.9 4.1 %collective-permute-start.15 = (bf16[2,12,8,24,128]{4,3,2,1,0:T(8,128)(2,1)}, bf16[2,12,8,24,128]{4,3,2,1,0:T(8,128)(2,1)}, u32[]{:S(2)}, u32[]{:S(2)}) collective-permute-start(bf16[2,12,8,24,128]{4,3,2,1,0:T(8,128)(2,1)} %get-tuple-element.23), channel_id=1, source_target_pairs={{0,8},{8,16},{16,24},{1,9},{9,17},{17,25},{2,10},{10,18},{18,26},{... | collective-permute-start | bytes 3538952 | tf_op jit(solution)/shard_map/ppermute | solution.py:89
  226.4 21.5 %all-to-all-start = ((f32[32,2,4]{2,1,0:T(2,128)}), f32[32,2,4]{2,1,0:T(2,128)S(1)}, u32[]{:S(2)}, u32[]{:S(2)}) async-start(f32[32,2,4]{2,1,0:T(2,128)} %copy.82), calls=%async_computation | async-start | bytes 65536 | tf_op jit(solution)/shard_map/all_to_all | solution.py:157
  254.7 4.1 %collective-permute-start.19 = (bf16[2,12,8,24,128]{4,3,2,1,0:T(8,128)(2,1)}, bf16[2,12,8,24,128]{4,3,2,1,0:T(8,128)(2,1)}, u32[]{:S(2)}, u32[]{:S(2)}) collective-permute-start(bf16[2,12,8,24,128]{4,3,2,1,0:T(8,128)(2,1)} %get-tuple-element.21), channel_id=1, source_target_pairs={{0,8},{8,16},{16,24},{1,9},{9,17},{17,25},{2,10},{10,18},{18,26},{... | collective-permute-start | bytes 3538952 | tf_op jit(solution)/shard_map/ppermute | solution.py:89
  261.3 10.2 %all-to-all-done = f32[32,2,4]{2,1,0:T(2,128)S(1)} async-done(((f32[32,2,4]{2,1,0:T(2,128)}), f32[32,2,4]{2,1,0:T(2,128)S(1)}, u32[]{:S(2)}, u32[]{:S(2)}) %all-to-all-start) | async-done | bytes 1056 | tf_op jit(solution)/shard_map/all_to_all | solution.py:157
  278.5 7.3 %collective-permute-start.17 = (bf16[2,12,8,8,128]{4,3,2,1,0:T(8,128)(2,1)S(1)}, bf16[2,12,8,8,128]{4,3,2,1,0:T(8,128)(2,1)S(1)}, u32[]{:S(2)}, u32[]{:S(2)}) collective-permute-start(bf16[2,12,8,8,128]{4,3,2,1,0:T(8,128)(2,1)S(1)} %get-tuple-element.27), channel_id=1, source_target_pairs={{0,1},{1,2},{2,3},{3,4},{4,5},{5,6},{6,7},{8,9},{9,10},{10,11},{11... | collective-permute-start | bytes 1179656 | tf_op jit(solution)/shard_map/ppermute | solution.py:89
  285.9 4.5 %fusion.60 = (bf16[2,12,8,24,128]{4,3,2,1,0:T(8,128)(2,1)S(1)}, f32[2,12,8,24,128]{4,3,2,1,0:T(8,128)}) fusion(bf16[2,12,8,24,128]{4,3,2,1,0:T(8,128)(2,1)} %collective-permute-done.19, bf16[2,12,8,24,128]{4,3,2,1,0:T(8,128)(2,1)} %collective-permute-done.18, f32[2,12,24,24,128]{4,3,2,1,0:T(8,128)} %bitcast.109), kind=kLoop, calls=%fused_computation.119 | loop fusion | flops 2949120 | bytes 8257536 | tf_op jit(solution)/shard_map/convert.3
  293.4 7.5 %collective-permute-start.21 = (bf16[2,12,8,8,128]{4,3,2,1,0:T(8,128)(2,1)}, bf16[2,12,8,8,128]{4,3,2,1,0:T(8,128)(2,1)}, u32[]{:S(2)}, u32[]{:S(2)}) collective-permute-start(bf16[2,12,8,8,128]{4,3,2,1,0:T(8,128)(2,1)} %get-tuple-element.25), channel_id=1, source_target_pairs={{0,1},{1,2},{2,3},{3,4},{4,5},{5,6},{6,7},{8,9},{9,10},{10,11},{11... | collective-permute-start | bytes 1179656 | tf_op jit(solution)/shard_map/ppermute | solution.py:89
  (152 shorter events, 99.5 us)
Async XLA Ops:
  1.9 104.5 %copy-start = (bf16[2,8,8,1536]{3,2,1,0:T(8,128)(2,1)S(1)}, bf16[2,8,8,1536]{3,2,1,0:T(8,128)(2,1)}, u32[]{:S(2)}) copy-start(bf16[2,8,8,1536]{3,2,1,0:T(8,128)(2,1)} %param.8) | copy-start | bytes 1179652
  1.9 24.9 %collective-permute-start.1 = (bf16[2,2,8,8,1536]{4,3,2,1,0:T(8,128)(2,1)S(1)}, bf16[2,2,8,8,1536]{4,3,2,1,0:T(8,128)(2,1)S(1)}, u32[]{:S(2)}, u32[]{:S(2)}) collective-permute-start(bf16[2,2,8,8,1536]{4,3,2,1,0:T(8,128)(2,1)S(1)} %pad_maximum_fusion.2), channel_id=1, source_target_pairs={{1,0},{2,1},{3,2},{4,3},{5,4},{6,5},{7,6},{9,8},{10,9},{11,10},{12... | collective-permute-start | bytes 2359304 | tf_op jit(solution)/shard_map/ppermute | solution.py:24
  4.8 23.2 %collective-permute-start = (bf16[2,2,8,8,1536]{4,3,2,1,0:T(8,128)(2,1)S(1)}, bf16[2,2,8,8,1536]{4,3,2,1,0:T(8,128)(2,1)S(1)}, u32[]{:S(2)}, u32[]{:S(2)}) collective-permute-start(bf16[2,2,8,8,1536]{4,3,2,1,0:T(8,128)(2,1)S(1)} %pad_maximum_fusion.2), channel_id=1, source_target_pairs={{0,1},{1,2},{2,3},{3,4},{4,5},{5,6},{6,7},{8,9},{9,10},{10,11},{11... | collective-permute-start | bytes 2359304 | tf_op jit(solution)/shard_map/ppermute | solution.py:22
  31.1 75.3 %collective-permute-start.3 = (bf16[2,2,8,24,1536]{4,3,2,1,0:T(8,128)(2,1)}, bf16[2,2,8,24,1536]{4,3,2,1,0:T(8,128)(2,1)}, u32[]{:S(2)}, u32[]{:S(2)}) collective-permute-start(bf16[2,2,8,24,1536]{4,3,2,1,0:T(8,128)(2,1)} %pad_maximum_fusion.1), channel_id=1, source_target_pairs={{8,0},{16,8},{24,16},{9,1},{17,9},{25,17},{10,2},{18,10},{26,18},{... | collective-permute-start | bytes 7077896 | tf_op jit(solution)/shard_map/ppermute | solution.py:24
  32.4 74.0 %collective-permute-start.2 = (bf16[2,2,8,24,1536]{4,3,2,1,0:T(8,128)(2,1)}, bf16[2,2,8,24,1536]{4,3,2,1,0:T(8,128)(2,1)}, u32[]{:S(2)}, u32[]{:S(2)}) collective-permute-start(bf16[2,2,8,24,1536]{4,3,2,1,0:T(8,128)(2,1)} %pad_maximum_fusion.1), channel_id=1, source_target_pairs={{0,8},{8,16},{16,24},{1,9},{9,17},{17,25},{2,10},{10,18},{18,26},{... | collective-permute-start | bytes 7077896 | tf_op jit(solution)/shard_map/ppermute | solution.py:22
  37.0 5.5 %collective-permute-start.4 = (f32[2,128]{1,0:T(2,128)S(1)}, f32[2,128]{1,0:T(2,128)S(1)}, u32[]{:S(2)}, u32[]{:S(2)}) collective-permute-start(f32[2,128]{1,0:T(2,128)S(1)} %dynamic_update_slice.5), channel_id=1, source_target_pairs={{0,32},{32,0},{64,96},{96,64},{128,160},{160,128},{192,224},{224,1... | collective-permute-start | bytes 3080 | tf_op jit(solution)/shard_map/ppermute | solution.py:35
  42.7 6.9 %collective-permute-start.5 = (f32[2,128]{1,0:T(2,128)S(1)}, f32[2,128]{1,0:T(2,128)S(1)}, u32[]{:S(2)}, u32[]{:S(2)}) collective-permute-start(f32[2,128]{1,0:T(2,128)S(1)} %add.178), channel_id=1, source_target_pairs={{0,64},{32,96},{64,0},{96,32},{128,192},{160,224},{192,128},{224,1... | collective-permute-start | bytes 3080 | tf_op jit(solution)/shard_map/ppermute | solution.py:35
  49.6 10.6 %collective-permute-start.6 = (f32[2,128]{1,0:T(2,128)S(1)}, f32[2,128]{1,0:T(2,128)S(1)}, u32[]{:S(2)}, u32[]{:S(2)}) collective-permute-start(f32[2,128]{1,0:T(2,128)S(1)} %add.179), channel_id=1, source_target_pairs={{0,128},{32,160},{64,192},{96,224},{128,0},{160,32},{192,64},{224,... | collective-permute-start | bytes 3080 | tf_op jit(solution)/shard_map/ppermute | solution.py:35
  60.2 17.3 %collective-permute-start.7 = (f32[2,128]{1,0:T(2,128)S(1)}, f32[2,128]{1,0:T(2,128)S(1)}, u32[]{:S(2)}, u32[]{:S(2)}) collective-permute-start(f32[2,128]{1,0:T(2,128)S(1)} %add.180), channel_id=1, source_target_pairs={{0,256},{32,288},{64,320},{96,352},{128,384},{160,416},{192,448},{... | collective-permute-start | bytes 3080 | tf_op jit(solution)/shard_map/ppermute | solution.py:35
  78.1 26.6 %collective-permute-start.8 = (f32[2,128]{1,0:T(2,128)}, f32[2,128]{1,0:T(2,128)}, u32[]{:S(2)}, u32[]{:S(2)}) collective-permute-start(f32[2,128]{1,0:T(2,128)} %add.181), channel_id=1, source_target_pairs={{0,512},{32,544},{64,576},{96,608},{128,640},{160,672},{192,704},{... | collective-permute-start | bytes 3080 | tf_op jit(solution)/shard_map/ppermute | solution.py:35
  179.1 5.5 %collective-permute-start.9 = (f32[2,128]{1,0:T(2,128)S(1)}, f32[2,128]{1,0:T(2,128)S(1)}, u32[]{:S(2)}, u32[]{:S(2)}) collective-permute-start(f32[2,128]{1,0:T(2,128)S(1)} %pad_maximum_fusion.4), channel_id=1, source_target_pairs={{0,1},{1,0},{2,3},{3,2},{4,5},{5,4},{6,7},{7,6},{8,9},{9,8},{10,11... | collective-permute-start | bytes 3080 | tf_op jit(solution)/shard_map/ppermute | solution.py:35
  185.3 7.0 %collective-permute-start.10 = (f32[2,128]{1,0:T(2,128)S(1)}, f32[2,128]{1,0:T(2,128)S(1)}, u32[]{:S(2)}, u32[]{:S(2)}) collective-permute-start(f32[2,128]{1,0:T(2,128)S(1)} %fusion.54), channel_id=1, source_target_pairs={{0,2},{1,3},{2,0},{3,1},{4,6},{5,7},{6,4},{7,5},{8,10},{9,11},{10,... | collective-permute-start | bytes 3080 | tf_op jit(solution)/shard_map/ppermute | solution.py:35
  193.0 7.0 %collective-permute-start.11 = (f32[2,128]{1,0:T(2,128)S(1)}, f32[2,128]{1,0:T(2,128)S(1)}, u32[]{:S(2)}, u32[]{:S(2)}) collective-permute-start(f32[2,128]{1,0:T(2,128)S(1)} %fusion.70), channel_id=1, source_target_pairs={{0,4},{1,5},{2,6},{3,7},{4,0},{5,1},{6,2},{7,3},{8,12},{9,13},{10,... | collective-permute-start | bytes 3080 | tf_op jit(solution)/shard_map/ppermute | solution.py:35
  200.0 8.8 %collective-permute-start.12 = (f32[2,128]{1,0:T(2,128)S(1)}, f32[2,128]{1,0:T(2,128)S(1)}, u32[]{:S(2)}, u32[]{:S(2)}) collective-permute-start(f32[2,128]{1,0:T(2,128)S(1)} %add.188), channel_id=1, source_target_pairs={{0,8},{8,0},{16,24},{24,16},{1,9},{9,1},{17,25},{25,17},{2,10},{10... | collective-permute-start | bytes 3080 | tf_op jit(solution)/shard_map/ppermute | solution.py:35
  208.7 5.5 %collective-permute-start.13 = (f32[2,128]{1,0:T(2,128)S(1)}, f32[2,128]{1,0:T(2,128)S(1)}, u32[]{:S(2)}, u32[]{:S(2)}) collective-permute-start(f32[2,128]{1,0:T(2,128)S(1)} %add.189), channel_id=1, source_target_pairs={{0,16},{8,24},{16,0},{24,8},{1,17},{9,25},{17,1},{25,9},{2,18},{10... | collective-permute-start | bytes 3080 | tf_op jit(solution)/shard_map/ppermute | solution.py:35
  219.6 52.4 %collective-permute-start.14 = (bf16[2,12,8,24,128]{4,3,2,1,0:T(8,128)(2,1)}, bf16[2,12,8,24,128]{4,3,2,1,0:T(8,128)(2,1)}, u32[]{:S(2)}, u32[]{:S(2)}) collective-permute-start(bf16[2,12,8,24,128]{4,3,2,1,0:T(8,128)(2,1)} %get-tuple-element.22), channel_id=1, source_target_pairs={{8,0},{16,8},{24,16},{9,1},{17,9},{25,17},{10,2},{18,10},{26,18},{... | collective-permute-start | bytes 3538952 | tf_op jit(solution)/shard_map/ppermute | solution.py:88
  220.9 51.1 %collective-permute-start.15 = (bf16[2,12,8,24,128]{4,3,2,1,0:T(8,128)(2,1)}, bf16[2,12,8,24,128]{4,3,2,1,0:T(8,128)(2,1)}, u32[]{:S(2)}, u32[]{:S(2)}) collective-permute-start(bf16[2,12,8,24,128]{4,3,2,1,0:T(8,128)(2,1)} %get-tuple-element.23), channel_id=1, source_target_pairs={{0,8},{8,16},{16,24},{1,9},{9,17},{17,25},{2,10},{10,18},{18,26},{... | collective-permute-start | bytes 3538952 | tf_op jit(solution)/shard_map/ppermute | solution.py:89
  226.4 45.0 %all-to-all-start = ((f32[32,2,4]{2,1,0:T(2,128)}), f32[32,2,4]{2,1,0:T(2,128)S(1)}, u32[]{:S(2)}, u32[]{:S(2)}) async-start(f32[32,2,4]{2,1,0:T(2,128)} %copy.82), calls=%async_computation | async-start | bytes 65536 | tf_op jit(solution)/shard_map/all_to_all | solution.py:157
  253.4 32.4 %collective-permute-start.18 = (bf16[2,12,8,24,128]{4,3,2,1,0:T(8,128)(2,1)}, bf16[2,12,8,24,128]{4,3,2,1,0:T(8,128)(2,1)}, u32[]{:S(2)}, u32[]{:S(2)}) collective-permute-start(bf16[2,12,8,24,128]{4,3,2,1,0:T(8,128)(2,1)} %get-tuple-element.20), channel_id=1, source_target_pairs={{8,0},{16,8},{24,16},{9,1},{17,9},{25,17},{10,2},{18,10},{26,18},{... | collective-permute-start | bytes 3538952 | tf_op jit(solution)/shard_map/ppermute | solution.py:88
  254.7 31.2 %collective-permute-start.19 = (bf16[2,12,8,24,128]{4,3,2,1,0:T(8,128)(2,1)}, bf16[2,12,8,24,128]{4,3,2,1,0:T(8,128)(2,1)}, u32[]{:S(2)}, u32[]{:S(2)}) collective-permute-start(bf16[2,12,8,24,128]{4,3,2,1,0:T(8,128)(2,1)} %get-tuple-element.21), channel_id=1, source_target_pairs={{0,8},{8,16},{16,24},{1,9},{9,17},{17,25},{2,10},{10,18},{18,26},{... | collective-permute-start | bytes 3538952 | tf_op jit(solution)/shard_map/ppermute | solution.py:89
  275.2 25.8 %collective-permute-start.16 = (bf16[2,12,8,8,128]{4,3,2,1,0:T(8,128)(2,1)S(1)}, bf16[2,12,8,8,128]{4,3,2,1,0:T(8,128)(2,1)S(1)}, u32[]{:S(2)}, u32[]{:S(2)}) collective-permute-start(bf16[2,12,8,8,128]{4,3,2,1,0:T(8,128)(2,1)S(1)} %get-tuple-element.26), channel_id=1, source_target_pairs={{1,0},{2,1},{3,2},{4,3},{5,4},{6,5},{7,6},{9,8},{10,9},{11,10},{12... | collective-permute-start | bytes 1179656 | tf_op jit(solution)/shard_map/ppermute | solution.py:88
  278.5 22.4 %collective-permute-start.17 = (bf16[2,12,8,8,128]{4,3,2,1,0:T(8,128)(2,1)S(1)}, bf16[2,12,8,8,128]{4,3,2,1,0:T(8,128)(2,1)S(1)}, u32[]{:S(2)}, u32[]{:S(2)}) collective-permute-start(bf16[2,12,8,8,128]{4,3,2,1,0:T(8,128)(2,1)S(1)} %get-tuple-element.27), channel_id=1, source_target_pairs={{0,1},{1,2},{2,3},{3,4},{4,5},{5,6},{6,7},{8,9},{9,10},{10,11},{11... | collective-permute-start | bytes 1179656 | tf_op jit(solution)/shard_map/ppermute | solution.py:89
  291.5 17.6 %collective-permute-start.20 = (bf16[2,12,8,8,128]{4,3,2,1,0:T(8,128)(2,1)}, bf16[2,12,8,8,128]{4,3,2,1,0:T(8,128)(2,1)}, u32[]{:S(2)}, u32[]{:S(2)}) collective-permute-start(bf16[2,12,8,8,128]{4,3,2,1,0:T(8,128)(2,1)} %get-tuple-element.24), channel_id=1, source_target_pairs={{1,0},{2,1},{3,2},{4,3},{5,4},{6,5},{7,6},{9,8},{10,9},{11,10},{12... | collective-permute-start | bytes 1179656 | tf_op jit(solution)/shard_map/ppermute | solution.py:88
  293.4 15.7 %collective-permute-start.21 = (bf16[2,12,8,8,128]{4,3,2,1,0:T(8,128)(2,1)}, bf16[2,12,8,8,128]{4,3,2,1,0:T(8,128)(2,1)}, u32[]{:S(2)}, u32[]{:S(2)}) collective-permute-start(bf16[2,12,8,8,128]{4,3,2,1,0:T(8,128)(2,1)} %get-tuple-element.25), channel_id=1, source_target_pairs={{0,1},{1,2},{2,3},{3,4},{4,5},{5,6},{6,7},{8,9},{9,10},{10,11},{11... | collective-permute-start | bytes 1179656 | tf_op jit(solution)/shard_map/ppermute | solution.py:89
  (24 other events, 502.7 us)

commit v2 on v1

--- a/solution.py
+++ b/solution.py
@@ -117,11 +117,10 @@
     head_count = windows.shape[0]
     share_len = q_gain.shape[0]
     head_size = share_len * lax.axis_size("fsdp")
-    gain_slots = jnp.zeros((2, head_size), jnp.float32)
-    gain_slots = lax.dynamic_update_slice_in_dim(
-        gain_slots, jnp.stack([q_gain, k_gain]), lax.axis_index("fsdp") * share_len, 1
-    )
-    gains = xor_sum(gain_slots, "fsdp")
+    owner_count = lax.axis_size("fsdp")
+    own_gains = jnp.broadcast_to(jnp.stack([q_gain, k_gain])[None], (owner_count, 2, share_len))
+    gathered_gains = lax.all_to_all(own_gains, "fsdp", 0, 0, tiled=True)
+    gains = gathered_gains.transpose(1, 0, 2).reshape(2, head_size)
     q_gain_all, k_gain_all = gains[0], gains[1]
     frame_count, row_count, col_count, feature_count = q_raw.shape
     score_scale = 1.0 / math.sqrt(head_size)

time: 315 us -> 286 us (0.908)
  starting transfers between devices: 141 us -> 93.9 us
  waiting for transfers between devices: 40 us -> 54.6 us
  local copies, waits for them, and re-layouts: 44.1 us -> 48 us
    ppermute x10 -> x5, starting transfers between devices: 73.1 us -> 14.8 us  [xor_sum(): lax.ppermute(cells, axis, [(i, i ^ step) for i in range(count)])]
    all_to_all x0 -> x1, starting transfers between devices: none -> 28.9 us  [body(): gathered_gains = lax.all_to_all(own_gains, 'fsdp', 0, 0, tiled=True)]
    all_to_all x0 -> x1, waiting for transfers between devices: none -> 19.5 us  [body(): gathered_gains = lax.all_to_all(own_gains, 'fsdp', 0, 0, tiled=True)]
    all_to_all x1, starting transfers between devices: 21.5 us -> 4.07 us  [body(): owned = lax.all_to_all(pieces, 'fsdp', 0, 0, tiled=True).sum(axis=0)]
    ppermute x10 -> x5, waiting for transfers between devices: 13.3 us -> 8.83 us  [xor_sum(): lax.ppermute(cells, axis, [(i, i ^ step) for i in range(count)])]
  transfers between devices with their start and end apart: 23 -> 19, of which waited for: 11 -> 8; matrix products, arithmetic and copies ran while one was open for 14% -> 17% of each run, Pallas kernels for 0% -> 0%
where the time goes in v2:
time: 286 us; the launch traced here: 282 us
  starting transfers between devices  93.9 us (33%)
  waiting for transfers between devices  54.6 us (19%)
  other arithmetic  50.8 us (18%)
  local copies, waits for them, and re-layouts  48 us (17%)
  matrix products  33.6 us (12%)
    dot_general x6, matrix products, product(): return jnp.einsum(form, left, right, preferred_element_type=jnp.float32)  33.6 us
    all_to_all x1, starting transfers between devices, body(): gathered_gains = lax.all_to_all(own_gains, 'fsdp', 0, 0, tiled=True)  28.9 us
    ppermute x4, starting transfers between devices, gathered(): lax.ppermute(tail.astype(jnp.bfloat16), axis, [(i, (i + 1) % count) for i...  23 us
    all_to_all x1, waiting for transfers between devices, body(): gathered_gains = lax.all_to_all(own_gains, 'fsdp', 0, 0, tiled=True)  19.5 us
    ppermute x2, waiting for transfers between devices, padded(): lax.ppermute(head, axis, [((i + 1) % count, i) for i in range(ends)])  15.3 us
    ppermute x5, starting transfers between devices, xor_sum(): lax.ppermute(cells, axis, [(i, i ^ step) for i in range(count)])  14.8 us
    another operation x4, other arithmetic  14.6 us
    ppermute x2, starting transfers between devices, padded(): lax.ppermute(tail, axis, [(i, (i + 1) % count) for i in range(ends)])  11.2 us
  transfers between devices with their start and end apart: 19, of which 8 were waited for; matrix products, arithmetic and copies ran while one was open for 17% of the time, Pallas kernels for 0%

profile of v2, /device:TPU:6, one launch (start us, length us, event | category | flops | bytes accessed | tf_op | source)
XLA Modules:
  0.0 282.1 jit_solution(14966057125612472945)
XLA Ops:
  4.8 6.7 %collective-permute-start = (bf16[2,2,8,8,1536]{4,3,2,1,0:T(8,128)(2,1)S(1)}, bf16[2,2,8,8,1536]{4,3,2,1,0:T(8,128)(2,1)S(1)}, u32[]{:S(2)}, u32[]{:S(2)}) collective-permute-start(bf16[2,2,8,8,1536]{4,3,2,1,0:T(8,128)(2,1)S(1)} %pad_maximum_fusion.2), channel_id=1, source_target_pairs={{0,1},{1,2},{2,3},{3,4},{4,5},{5,6},{6,7},{8,9},{9,10},{10,11},{11... | collective-permute-start | bytes 2359304 | tf_op jit(solution)/shard_map/ppermute | solution.py:22
  11.5 15.3 %collective-permute-done.1 = bf16[2,2,8,8,1536]{4,3,2,1,0:T(8,128)(2,1)S(1)} collective-permute-done((bf16[2,2,8,8,1536]{4,3,2,1,0:T(8,128)(2,1)S(1)}, bf16[2,2,8,8,1536]{4,3,2,1,0:T(8,128)(2,1)S(1)}, u32[]{:S(2)}, u32[]{:S(2)}) %collective-permute-start.1) | collective-permute-done | bytes 786464 | tf_op jit(solution)/shard_map/ppermute | solution.py:24
  32.4 4.5 %collective-permute-start.2 = (bf16[2,2,8,24,1536]{4,3,2,1,0:T(8,128)(2,1)}, bf16[2,2,8,24,1536]{4,3,2,1,0:T(8,128)(2,1)}, u32[]{:S(2)}, u32[]{:S(2)}) collective-permute-start(bf16[2,2,8,24,1536]{4,3,2,1,0:T(8,128)(2,1)} %pad_maximum_fusion.1), channel_id=1, source_target_pairs={{0,8},{8,16},{16,24},{1,9},{9,17},{17,25},{2,10},{10,18},{18,26},{... | collective-permute-start | bytes 7077896 | tf_op jit(solution)/shard_map/ppermute | solution.py:22
  37.5 28.9 %all-to-all-start = ((f32[32,2,4]{2,1,0:T(2,128)}), f32[32,2,4]{2,1,0:T(2,128)}, u32[]{:S(2)}, u32[]{:S(2)}) async-start(f32[32,2,4]{2,1,0:T(2,128)} %broadcast_in_dim.11), calls=%async_computation | async-start | bytes 65536 | tf_op jit(solution)/shard_map/all_to_all | solution.py:122
  69.9 19.5 %all-to-all-done = f32[32,2,4]{2,1,0:T(2,128)} async-done(((f32[32,2,4]{2,1,0:T(2,128)}), f32[32,2,4]{2,1,0:T(2,128)}, u32[]{:S(2)}, u32[]{:S(2)}) %all-to-all-start) | async-done | bytes 1056 | tf_op jit(solution)/shard_map/all_to_all | solution.py:122
  98.3 3.9 %fusion.12 = f32[1,2,24,24,1536]{4,3,2,1,0:T(8,128)} fusion(bf16[2,2,24,24,1536]{4,3,2,1,0:T(8,128)(2,1)S(1)} %pad_maximum_fusion), kind=kLoop, calls=%fused_computation.21 | loop fusion | flops 3538944 | bytes 10616832 | tf_op jit(solution)/shard_map/mul | solution.py:47
  102.2 5.1 %slice_convert_fusion = (f32[1,2,24,24,1536]{4,3,2,1,0:T(8,128)}, bf16[1,2,24,24,1536]{4,3,2,1,0:T(8,128)(2,1)}) fusion(bf16[2,2,24,24,1536]{4,3,2,1,0:T(8,128)(2,1)S(1)} %pad_maximum_fusion), kind=kLoop, calls=%fused_computation.8 | loop fusion | flops 1769472 | bytes 17694720 | tf_op jit(solution)/shard_map/convert_element_type | solution.py:45
  107.3 9.1 %mul.194 = f32[2,24,24,12,128]{4,3,2,1,0:T(8,128)} reshape(f32[1,2,24,24,1536]{4,3,2,1,0:T(8,128)} %fusion.12) | data formatting | bytes 14155776 | tf_op jit(solution)/shard_map/mul | solution.py:47
  116.4 6.2 %reduce_sum.91 = f32[2,24,24,12]{3,2,1,0:T(8,128)S(1)} reduce(f32[2,24,24,12,128]{4,3,2,1,0:T(8,128)} %mul.194, f32[]{:T(128)} %constant.88.clone.1), dimensions={4}, to_apply=%region_1.0 | reduce | flops 1755648 | bytes 7133188 | tf_op jit(solution)/shard_map/reduce_sum | solution.py:47
  123.2 9.1 %reshape.207 = f32[2,576,12,128]{3,2,1,0:T(8,128)} reshape(f32[1,2,24,24,1536]{4,3,2,1,0:T(8,128)} %get-tuple-element.20) | data formatting | bytes 14155776 | tf_op jit(solution)/shard_map/convert_element_type | solution.py:45
  132.3 7.4 %reshape_squeeze.3 = bf16[2,576,12,128]{3,2,1,0:T(8,128)(2,1)} reshape(bf16[1,2,24,24,1536]{4,3,2,1,0:T(8,128)(2,1)} %get-tuple-element.21) | data formatting | bytes 7077888 | tf_op jit(solution)/shard_map/reshape;squeeze | solution.py:140
  139.7 8.1 %fusion.3 = (f32[2,12,64]{2,1,0:T(8,128)S(1)}, f32[2,12,64,576]{3,2,1,0:T(8,128)S(1)}) fusion(pred[12,576]{1,0:T(8,128)(4,1)S(1)} %copy-done.9, f32[2,576,12,128]{3,2,1,0:T(8,128)} %reshape.207, f32[128]{0:T(128)S(1)} %copy-done.11, f32[2,576,12]{1,2,0:T(8,128)S(1)} %reshape.210, f32[128]{0:T(128)S(1)} %copy-done.14, f32[2,64,12]{1,2,0:T(8,128)S(1)} %copy.59, ...), kind=kOutput, calls=%fused_computation.11 | convolution fusion | flops 235043328 | bytes 11478784 | tf_op jit(solution)/shard_map/vmap(qhc,mhc->hqm)/dot_general | solution.py:41
  154.3 7.3 %fusion = (f32[128]{0:T(128)S(1)}, f32[2,12,576,128]{3,2,1,0:T(8,128)}) fusion(f32[2,576,12,128]{3,2,1,0:T(8,128)S(1)} %bitcast.97, f32[2,576,12]{1,2,0:T(8,128)S(1)} %reshape.210, bf16[2,12,64,576]{3,2,1,0:T(8,128)(2,1)S(1)} %fusion.1, f32[128]{0:T(128)S(1)} %copy-done.14, f32[2,64,12]{1,2,0:T(8,128)S(1)} %copy.59, f32[2,64,12,128]{3,2,1,0:T(8,128)S(1)} %reshape.198), kind=kOutput, calls=%fused_computation.2 | convolution fusion | flops 234160000 | bytes 16774144 | tf_op jit(solution)/shard_map/vmap(hqm,qhc->hmc)/dot_general | solution.py:41
  161.6 5.8 %multiply_reduce_fusion.1 = (f32[128]{0:T(128)S(1)}, f32[2,64,12]{1,2,0:T(8,128)}, f32[2,12,128,64]{2,3,1,0:T(8,128)S(1)}) fusion(f32[2,64,12]{1,2,0:T(8,128)S(1)} %copy.59, f32[2,64,12,128]{3,2,1,0:T(8,128)S(1)} %reshape.198, f32[128]{0:T(128)S(1)} %copy-done.18, bf16[2,12,64,576]{3,2,1,0:T(8,128)(2,1)S(1)} %fusion.1, ...), kind=kOutput, calls=%fused_computation.47 | convolution fusion | flops 233175424 | bytes 10489344 | tf_op jit(solution)/shard_map/vmap(hqm,mhc->qhc)/dot_general | solution.py:41
  181.2 5.9 %collective-permute-start.6 = (f32[2,128]{1,0:T(2,128)S(1)}, f32[2,128]{1,0:T(2,128)S(1)}, u32[]{:S(2)}, u32[]{:S(2)}) collective-permute-start(f32[2,128]{1,0:T(2,128)S(1)} %fusion.70), channel_id=1, source_target_pairs={{0,4},{1,5},{2,6},{3,7},{4,0},{5,1},{6,2},{7,3},{8,12},{9,13},{10,... | collective-permute-start | bytes 3080 | tf_op jit(solution)/shard_map/ppermute | solution.py:35
  190.7 6.7 %fusion.19 = f32[2,12,576,128]{3,2,1,0:T(8,128)} fusion(bf16[2,64,12,128]{3,2,1,0:T(8,128)(2,1)S(1)} %reshape.200, f32[2,12,64,576]{3,2,1,0:T(8,128)} %copy-done.2, f32[2,12,64]{2,1,0:T(8,128)} %copy-done.15, pred[12,576]{1,0:T(8,128)(4,1)} %and_and_fusion), kind=kOutput, calls=%fused_computation.26 | convolution fusion | flops 230031360 | bytes 11023104 | tf_op jit(solution)/shard_map/vmap(hqm,qhc->hmc)/dot_general | solution.py:41
  209.6 4.1 %collective-permute-start.10 = (bf16[2,12,8,24,128]{4,3,2,1,0:T(8,128)(2,1)}, bf16[2,12,8,24,128]{4,3,2,1,0:T(8,128)(2,1)}, u32[]{:S(2)}, u32[]{:S(2)}) collective-permute-start(bf16[2,12,8,24,128]{4,3,2,1,0:T(8,128)(2,1)} %get-tuple-element.25), channel_id=1, source_target_pairs={{0,8},{8,16},{16,24},{1,9},{9,17},{17,25},{2,10},{10,18},{18,26},{... | collective-permute-start | bytes 3538952 | tf_op jit(solution)/shard_map/ppermute | solution.py:89
  215.1 4.1 %all-to-all-start.1 = ((f32[32,2,4]{2,1,0:T(2,128)}), f32[32,2,4]{2,1,0:T(2,128)S(1)}, u32[]{:S(2)}, u32[]{:S(2)}) async-start(f32[32,2,4]{2,1,0:T(2,128)} %copy.82), calls=%async_computation.1 | async-start | bytes 65536 | tf_op jit(solution)/shard_map/all_to_all | solution.py:156
  219.2 3.6 %convert.20 = bf16[2,12,24,24,128]{4,3,2,1,0:T(8,128)(2,1)S(1)} convert(f32[2,12,24,24,128]{4,3,2,1,0:T(8,128)} %bitcast.103) | non-fusion elementwise | flops 1769472 | bytes 10616832 | tf_op jit(solution)/shard_map/convert.5
  225.9 4.1 %collective-permute-start.14 = (bf16[2,12,8,24,128]{4,3,2,1,0:T(8,128)(2,1)}, bf16[2,12,8,24,128]{4,3,2,1,0:T(8,128)(2,1)}, u32[]{:S(2)}, u32[]{:S(2)}) collective-permute-start(bf16[2,12,8,24,128]{4,3,2,1,0:T(8,128)(2,1)} %get-tuple-element.23), channel_id=1, source_target_pairs={{0,8},{8,16},{16,24},{1,9},{9,17},{17,25},{2,10},{10,18},{18,26},{... | collective-permute-start | bytes 3538952 | tf_op jit(solution)/shard_map/ppermute | solution.py:89
  232.5 9.7 %all-to-all-done.1 = f32[32,2,4]{2,1,0:T(2,128)S(1)} async-done(((f32[32,2,4]{2,1,0:T(2,128)}), f32[32,2,4]{2,1,0:T(2,128)S(1)}, u32[]{:S(2)}, u32[]{:S(2)}) %all-to-all-start.1) | async-done | bytes 1056 | tf_op jit(solution)/shard_map/all_to_all | solution.py:156
  249.3 7.3 %collective-permute-start.12 = (bf16[2,12,8,8,128]{4,3,2,1,0:T(8,128)(2,1)S(1)}, bf16[2,12,8,8,128]{4,3,2,1,0:T(8,128)(2,1)S(1)}, u32[]{:S(2)}, u32[]{:S(2)}) collective-permute-start(bf16[2,12,8,8,128]{4,3,2,1,0:T(8,128)(2,1)S(1)} %get-tuple-element.29), channel_id=1, source_target_pairs={{0,1},{1,2},{2,3},{3,4},{4,5},{5,6},{6,7},{8,9},{9,10},{10,11},{11... | collective-permute-start | bytes 1179656 | tf_op jit(solution)/shard_map/ppermute | solution.py:89
  256.6 4.5 %fusion.60 = (bf16[2,12,8,24,128]{4,3,2,1,0:T(8,128)(2,1)S(1)}, f32[2,12,8,24,128]{4,3,2,1,0:T(8,128)}) fusion(bf16[2,12,8,24,128]{4,3,2,1,0:T(8,128)(2,1)} %collective-permute-done.14, bf16[2,12,8,24,128]{4,3,2,1,0:T(8,128)(2,1)} %collective-permute-done.13, f32[2,12,24,24,128]{4,3,2,1,0:T(8,128)} %bitcast.104), kind=kLoop, calls=%fused_computation.118 | loop fusion | flops 2949120 | bytes 8257536 | tf_op jit(solution)/shard_map/convert.3
  264.2 7.5 %collective-permute-start.16 = (bf16[2,12,8,8,128]{4,3,2,1,0:T(8,128)(2,1)}, bf16[2,12,8,8,128]{4,3,2,1,0:T(8,128)(2,1)}, u32[]{:S(2)}, u32[]{:S(2)}) collective-permute-start(bf16[2,12,8,8,128]{4,3,2,1,0:T(8,128)(2,1)} %get-tuple-element.27), channel_id=1, source_target_pairs={{0,1},{1,2},{2,3},{3,4},{4,5},{5,6},{6,7},{8,9},{9,10},{10,11},{11... | collective-permute-start | bytes 1179656 | tf_op jit(solution)/shard_map/ppermute | solution.py:89
  (139 shorter events, 86.5 us)
Async XLA Ops:
  0.7 65.7 %copy-start.4 = (bf16[2,8,8,1536]{3,2,1,0:T(8,128)(2,1)S(1)}, bf16[2,8,8,1536]{3,2,1,0:T(8,128)(2,1)}, u32[]{:S(2)}) copy-start(bf16[2,8,8,1536]{3,2,1,0:T(8,128)(2,1)} %param.7) | copy-start | bytes 1179652
  0.7 66.2 %copy-start.19 = (s32[12,2]{0,1:T(2,128)S(1)}, s32[12,2]{0,1:T(2,128)}, u32[]{:S(2)}) copy-start(s32[12,2]{0,1:T(2,128)} %param.13) | copy-start | bytes 292
  1.9 92.9 %copy-start = (bf16[2,8,8,1536]{3,2,1,0:T(8,128)(2,1)S(1)}, bf16[2,8,8,1536]{3,2,1,0:T(8,128)(2,1)}, u32[]{:S(2)}) copy-start(bf16[2,8,8,1536]{3,2,1,0:T(8,128)(2,1)} %param.8) | copy-start | bytes 1179652
  1.9 92.9 %copy-start.3 = (bf16[2,8,8,1536]{3,2,1,0:T(8,128)(2,1)S(1)}, bf16[2,8,8,1536]{3,2,1,0:T(8,128)(2,1)}, u32[]{:S(2)}) copy-start(bf16[2,8,8,1536]{3,2,1,0:T(8,128)(2,1)} %param.9) | copy-start | bytes 1179652
  1.9 24.9 %collective-permute-start.1 = (bf16[2,2,8,8,1536]{4,3,2,1,0:T(8,128)(2,1)S(1)}, bf16[2,2,8,8,1536]{4,3,2,1,0:T(8,128)(2,1)S(1)}, u32[]{:S(2)}, u32[]{:S(2)}) collective-permute-start(bf16[2,2,8,8,1536]{4,3,2,1,0:T(8,128)(2,1)S(1)} %pad_maximum_fusion.2), channel_id=1, source_target_pairs={{1,0},{2,1},{3,2},{4,3},{5,4},{6,5},{7,6},{9,8},{10,9},{11,10},{12... | collective-permute-start | bytes 2359304 | tf_op jit(solution)/shard_map/ppermute | solution.py:24
  4.8 23.2 %collective-permute-start = (bf16[2,2,8,8,1536]{4,3,2,1,0:T(8,128)(2,1)S(1)}, bf16[2,2,8,8,1536]{4,3,2,1,0:T(8,128)(2,1)S(1)}, u32[]{:S(2)}, u32[]{:S(2)}) collective-permute-start(bf16[2,2,8,8,1536]{4,3,2,1,0:T(8,128)(2,1)S(1)} %pad_maximum_fusion.2), channel_id=1, source_target_pairs={{0,1},{1,2},{2,3},{3,4},{4,5},{5,6},{6,7},{8,9},{9,10},{10,11},{11... | collective-permute-start | bytes 2359304 | tf_op jit(solution)/shard_map/ppermute | solution.py:22
  28.0 39.5 %copy-start.5 = (bf16[2,2,8,8,1536]{4,3,2,1,0:T(8,128)(2,1)}, bf16[2,2,8,8,1536]{4,3,2,1,0:T(8,128)(2,1)S(1)}, u32[]{:S(2)}) copy-start(bf16[2,2,8,8,1536]{4,3,2,1,0:T(8,128)(2,1)S(1)} %collective-permute-done) | copy-start | bytes 2359300
  31.1 63.7 %collective-permute-start.3 = (bf16[2,2,8,24,1536]{4,3,2,1,0:T(8,128)(2,1)}, bf16[2,2,8,24,1536]{4,3,2,1,0:T(8,128)(2,1)}, u32[]{:S(2)}, u32[]{:S(2)}) collective-permute-start(bf16[2,2,8,24,1536]{4,3,2,1,0:T(8,128)(2,1)} %pad_maximum_fusion.1), channel_id=1, source_target_pairs={{8,0},{16,8},{24,16},{9,1},{17,9},{25,17},{10,2},{18,10},{26,18},{... | collective-permute-start | bytes 7077896 | tf_op jit(solution)/shard_map/ppermute | solution.py:24
  32.4 62.4 %collective-permute-start.2 = (bf16[2,2,8,24,1536]{4,3,2,1,0:T(8,128)(2,1)}, bf16[2,2,8,24,1536]{4,3,2,1,0:T(8,128)(2,1)}, u32[]{:S(2)}, u32[]{:S(2)}) collective-permute-start(bf16[2,2,8,24,1536]{4,3,2,1,0:T(8,128)(2,1)} %pad_maximum_fusion.1), channel_id=1, source_target_pairs={{0,8},{8,16},{16,24},{1,9},{9,17},{17,25},{2,10},{10,18},{18,26},{... | collective-permute-start | bytes 7077896 | tf_op jit(solution)/shard_map/ppermute | solution.py:22
  37.5 51.9 %all-to-all-start = ((f32[32,2,4]{2,1,0:T(2,128)}), f32[32,2,4]{2,1,0:T(2,128)}, u32[]{:S(2)}, u32[]{:S(2)}) async-start(f32[32,2,4]{2,1,0:T(2,128)} %broadcast_in_dim.11), calls=%async_computation | async-start | bytes 65536 | tf_op jit(solution)/shard_map/all_to_all | solution.py:122
  167.4 5.5 %collective-permute-start.4 = (f32[2,128]{1,0:T(2,128)S(1)}, f32[2,128]{1,0:T(2,128)S(1)}, u32[]{:S(2)}, u32[]{:S(2)}) collective-permute-start(f32[2,128]{1,0:T(2,128)S(1)} %pad_maximum_fusion.4), channel_id=1, source_target_pairs={{0,1},{1,0},{2,3},{3,2},{4,5},{5,4},{6,7},{7,6},{8,9},{9,8},{10,11... | collective-permute-start | bytes 3080 | tf_op jit(solution)/shard_map/ppermute | solution.py:35
  173.5 7.0 %collective-permute-start.5 = (f32[2,128]{1,0:T(2,128)S(1)}, f32[2,128]{1,0:T(2,128)S(1)}, u32[]{:S(2)}, u32[]{:S(2)}) collective-permute-start(f32[2,128]{1,0:T(2,128)S(1)} %fusion.54), channel_id=1, source_target_pairs={{0,2},{1,3},{2,0},{3,1},{4,6},{5,7},{6,4},{7,5},{8,10},{9,11},{10,... | collective-permute-start | bytes 3080 | tf_op jit(solution)/shard_map/ppermute | solution.py:35
  181.2 7.5 %collective-permute-start.6 = (f32[2,128]{1,0:T(2,128)S(1)}, f32[2,128]{1,0:T(2,128)S(1)}, u32[]{:S(2)}, u32[]{:S(2)}) collective-permute-start(f32[2,128]{1,0:T(2,128)S(1)} %fusion.70), channel_id=1, source_target_pairs={{0,4},{1,5},{2,6},{3,7},{4,0},{5,1},{6,2},{7,3},{8,12},{9,13},{10,... | collective-permute-start | bytes 3080 | tf_op jit(solution)/shard_map/ppermute | solution.py:35
  188.6 8.7 %collective-permute-start.7 = (f32[2,128]{1,0:T(2,128)S(1)}, f32[2,128]{1,0:T(2,128)S(1)}, u32[]{:S(2)}, u32[]{:S(2)}) collective-permute-start(f32[2,128]{1,0:T(2,128)S(1)} %add.163), channel_id=1, source_target_pairs={{0,8},{8,0},{16,24},{24,16},{1,9},{9,1},{17,25},{25,17},{2,10},{10... | collective-permute-start | bytes 3080 | tf_op jit(solution)/shard_map/ppermute | solution.py:35
  197.4 5.5 %collective-permute-start.8 = (f32[2,128]{1,0:T(2,128)S(1)}, f32[2,128]{1,0:T(2,128)S(1)}, u32[]{:S(2)}, u32[]{:S(2)}) collective-permute-start(f32[2,128]{1,0:T(2,128)S(1)} %add.164), channel_id=1, source_target_pairs={{0,16},{8,24},{16,0},{24,8},{1,17},{9,25},{17,1},{25,9},{2,18},{10... | collective-permute-start | bytes 3080 | tf_op jit(solution)/shard_map/ppermute | solution.py:35
  208.3 34.5 %collective-permute-start.9 = (bf16[2,12,8,24,128]{4,3,2,1,0:T(8,128)(2,1)}, bf16[2,12,8,24,128]{4,3,2,1,0:T(8,128)(2,1)}, u32[]{:S(2)}, u32[]{:S(2)}) collective-permute-start(bf16[2,12,8,24,128]{4,3,2,1,0:T(8,128)(2,1)} %get-tuple-element.24), channel_id=1, source_target_pairs={{8,0},{16,8},{24,16},{9,1},{17,9},{25,17},{10,2},{18,10},{26,18},{... | collective-permute-start | bytes 3538952 | tf_op jit(solution)/shard_map/ppermute | solution.py:88
  209.6 33.2 %collective-permute-start.10 = (bf16[2,12,8,24,128]{4,3,2,1,0:T(8,128)(2,1)}, bf16[2,12,8,24,128]{4,3,2,1,0:T(8,128)(2,1)}, u32[]{:S(2)}, u32[]{:S(2)}) collective-permute-start(bf16[2,12,8,24,128]{4,3,2,1,0:T(8,128)(2,1)} %get-tuple-element.25), channel_id=1, source_target_pairs={{0,8},{8,16},{16,24},{1,9},{9,17},{17,25},{2,10},{10,18},{18,26},{... | collective-permute-start | bytes 3538952 | tf_op jit(solution)/shard_map/ppermute | solution.py:89
  215.1 27.1 %all-to-all-start.1 = ((f32[32,2,4]{2,1,0:T(2,128)}), f32[32,2,4]{2,1,0:T(2,128)S(1)}, u32[]{:S(2)}, u32[]{:S(2)}) async-start(f32[32,2,4]{2,1,0:T(2,128)} %copy.82), calls=%async_computation.1 | async-start | bytes 65536 | tf_op jit(solution)/shard_map/all_to_all | solution.py:156
  224.6 32.0 %collective-permute-start.13 = (bf16[2,12,8,24,128]{4,3,2,1,0:T(8,128)(2,1)}, bf16[2,12,8,24,128]{4,3,2,1,0:T(8,128)(2,1)}, u32[]{:S(2)}, u32[]{:S(2)}) collective-permute-start(bf16[2,12,8,24,128]{4,3,2,1,0:T(8,128)(2,1)} %get-tuple-element.22), channel_id=1, source_target_pairs={{8,0},{16,8},{24,16},{9,1},{17,9},{25,17},{10,2},{18,10},{26,18},{... | collective-permute-start | bytes 3538952 | tf_op jit(solution)/shard_map/ppermute | solution.py:88
  225.9 30.7 %collective-permute-start.14 = (bf16[2,12,8,24,128]{4,3,2,1,0:T(8,128)(2,1)}, bf16[2,12,8,24,128]{4,3,2,1,0:T(8,128)(2,1)}, u32[]{:S(2)}, u32[]{:S(2)}) collective-permute-start(bf16[2,12,8,24,128]{4,3,2,1,0:T(8,128)(2,1)} %get-tuple-element.23), channel_id=1, source_target_pairs={{0,8},{8,16},{16,24},{1,9},{9,17},{17,25},{2,10},{10,18},{18,26},{... | collective-permute-start | bytes 3538952 | tf_op jit(solution)/shard_map/ppermute | solution.py:89
  245.9 25.8 %collective-permute-start.11 = (bf16[2,12,8,8,128]{4,3,2,1,0:T(8,128)(2,1)S(1)}, bf16[2,12,8,8,128]{4,3,2,1,0:T(8,128)(2,1)S(1)}, u32[]{:S(2)}, u32[]{:S(2)}) collective-permute-start(bf16[2,12,8,8,128]{4,3,2,1,0:T(8,128)(2,1)S(1)} %get-tuple-element.28), channel_id=1, source_target_pairs={{1,0},{2,1},{3,2},{4,3},{5,4},{6,5},{7,6},{9,8},{10,9},{11,10},{12... | collective-permute-start | bytes 1179656 | tf_op jit(solution)/shard_map/ppermute | solution.py:88
  249.3 22.4 %collective-permute-start.12 = (bf16[2,12,8,8,128]{4,3,2,1,0:T(8,128)(2,1)S(1)}, bf16[2,12,8,8,128]{4,3,2,1,0:T(8,128)(2,1)S(1)}, u32[]{:S(2)}, u32[]{:S(2)}) collective-permute-start(bf16[2,12,8,8,128]{4,3,2,1,0:T(8,128)(2,1)S(1)} %get-tuple-element.29), channel_id=1, source_target_pairs={{0,1},{1,2},{2,3},{3,4},{4,5},{5,6},{6,7},{8,9},{9,10},{10,11},{11... | collective-permute-start | bytes 1179656 | tf_op jit(solution)/shard_map/ppermute | solution.py:89
  262.2 17.6 %collective-permute-start.15 = (bf16[2,12,8,8,128]{4,3,2,1,0:T(8,128)(2,1)}, bf16[2,12,8,8,128]{4,3,2,1,0:T(8,128)(2,1)}, u32[]{:S(2)}, u32[]{:S(2)}) collective-permute-start(bf16[2,12,8,8,128]{4,3,2,1,0:T(8,128)(2,1)} %get-tuple-element.26), channel_id=1, source_target_pairs={{1,0},{2,1},{3,2},{4,3},{5,4},{6,5},{7,6},{9,8},{10,9},{11,10},{12... | collective-permute-start | bytes 1179656 | tf_op jit(solution)/shard_map/ppermute | solution.py:88
  264.2 15.7 %collective-permute-start.16 = (bf16[2,12,8,8,128]{4,3,2,1,0:T(8,128)(2,1)}, bf16[2,12,8,8,128]{4,3,2,1,0:T(8,128)(2,1)}, u32[]{:S(2)}, u32[]{:S(2)}) collective-permute-start(bf16[2,12,8,8,128]{4,3,2,1,0:T(8,128)(2,1)} %get-tuple-element.27), channel_id=1, source_target_pairs={{0,1},{1,2},{2,3},{3,4},{4,5},{5,6},{6,7},{8,9},{9,10},{10,11},{11... | collective-permute-start | bytes 1179656 | tf_op jit(solution)/shard_map/ppermute | solution.py:89
  (20 other events, 235.8 us)

commit v3 on v2

--- a/solution.py
+++ b/solution.py
@@ -4,6 +4,7 @@
 import jax.numpy as jnp
 from jax import lax
 from jax.sharding import PartitionSpec as P
+
 
 TILE = 8
 
@@ -47,13 +48,6 @@
     inverse = lax.rsqrt(jnp.mean(floats * floats, axis=-1, keepdims=True) + NORM_EPS)
     normed = floats * inverse
     return (normed, inverse, (normed * norm_gain).astype(jnp.bfloat16))
-
-
-def norm_backward(upstream, normed, inverse, norm_gain):
-    gain_part = jnp.sum(upstream * normed, axis=tuple(range(upstream.ndim - 1)))
-    scaled = upstream * norm_gain
-    raw_grad = inverse * (scaled - normed * jnp.mean(scaled * normed, axis=-1, keepdims=True))
-    return (raw_grad, gain_part)
 
 
 def open_pairs(windows, tile_size):
@@ -113,7 +107,7 @@
     return (output, query_grad, key_part, value_part)
 
 
-def body(q_raw, k_raw, values, d_out, q_gain, k_gain, windows):
+def body_steps(q_raw, k_raw, values, d_out, q_gain, k_gain, windows):
     head_count = windows.shape[0]
     share_len = q_gain.shape[0]
     head_size = share_len * lax.axis_size("fsdp")
@@ -122,7 +116,7 @@
     gathered_gains = lax.all_to_all(own_gains, "fsdp", 0, 0, tiled=True)
     gains = gathered_gains.transpose(1, 0, 2).reshape(2, head_size)
     q_gain_all, k_gain_all = gains[0], gains[1]
-    frame_count, row_count, col_count, feature_count = q_raw.shape
+    frame_count, row_count, col_count, _ = q_raw.shape
     score_scale = 1.0 / math.sqrt(head_size)
     sides = (("tx", 3), ("ty", 2))
     arrived = padded(jnp.stack([k_raw, values]), sides, TILE)
@@ -176,8 +170,12 @@
 
 
 def solution(mesh):
+    return shard_mapped(mesh)
+
+
+def shard_mapped(mesh):
     return jax.shard_map(
-        body,
+        body_steps,
         mesh=mesh,
         in_specs=(
             P("fsdp", "ty", "tx", None),

time: 286 us -> 286 us (level)
  no operation moved by 1% of the time
where the time goes in v3:
time: 286 us; the launch traced here: 282 us
  starting transfers between devices  93.9 us (33%)
  waiting for transfers between devices  54.6 us (19%)
  other arithmetic  50.8 us (18%)
  local copies, waits for them, and re-layouts  48 us (17%)
  matrix products  33.6 us (12%)
    dot_general x6, matrix products, product(): return jnp.einsum(form, left, right, preferred_element_type=jnp.float32)  33.6 us
    all_to_all x1, starting transfers between devices, body_steps(): gathered_gains = lax.all_to_all(own_gains, 'fsdp', 0, 0, tiled=True)  28.9 us
    ppermute x4, starting transfers between devices, gathered(): lax.ppermute(tail.astype(jnp.bfloat16), axis, [(i, (i + 1) % count) for i...  23 us
    all_to_all x1, waiting for transfers between devices, body_steps(): gathered_gains = lax.all_to_all(own_gains, 'fsdp', 0, 0, tiled=True)  19.5 us
    ppermute x2, waiting for transfers between devices, padded(): lax.ppermute(head, axis, [((i + 1) % count, i) for i in range(ends)])  15.3 us
    ppermute x5, starting transfers between devices, xor_sum(): lax.ppermute(cells, axis, [(i, i ^ step) for i in range(count)])  14.8 us
    another operation x4, other arithmetic  14.6 us
    ppermute x2, starting transfers between devices, padded(): lax.ppermute(tail, axis, [(i, (i + 1) % count) for i in range(ends)])  11.2 us
  transfers between devices with their start and end apart: 19, of which 8 were waited for; matrix products, arithmetic and copies ran while one was open for 17% of the time, Pallas kernels for 0%

profile of v3, /device:TPU:6, one launch (start us, length us, event | category | flops | bytes accessed | tf_op | source)
XLA Modules:
  0.0 282.1 jit_solution(14966057125612472945)
XLA Ops:
  4.8 6.7 %collective-permute-start = (bf16[2,2,8,8,1536]{4,3,2,1,0:T(8,128)(2,1)S(1)}, bf16[2,2,8,8,1536]{4,3,2,1,0:T(8,128)(2,1)S(1)}, u32[]{:S(2)}, u32[]{:S(2)}) collective-permute-start(bf16[2,2,8,8,1536]{4,3,2,1,0:T(8,128)(2,1)S(1)} %pad_maximum_fusion.2), channel_id=1, source_target_pairs={{0,1},{1,2},{2,3},{3,4},{4,5},{5,6},{6,7},{8,9},{9,10},{10,11},{11... | collective-permute-start | bytes 2359304 | tf_op jit(solution)/shard_map/ppermute | solution.py:23
  11.5 15.3 %collective-permute-done.1 = bf16[2,2,8,8,1536]{4,3,2,1,0:T(8,128)(2,1)S(1)} collective-permute-done((bf16[2,2,8,8,1536]{4,3,2,1,0:T(8,128)(2,1)S(1)}, bf16[2,2,8,8,1536]{4,3,2,1,0:T(8,128)(2,1)S(1)}, u32[]{:S(2)}, u32[]{:S(2)}) %collective-permute-start.1) | collective-permute-done | bytes 786464 | tf_op jit(solution)/shard_map/ppermute | solution.py:25
  32.4 4.5 %collective-permute-start.2 = (bf16[2,2,8,24,1536]{4,3,2,1,0:T(8,128)(2,1)}, bf16[2,2,8,24,1536]{4,3,2,1,0:T(8,128)(2,1)}, u32[]{:S(2)}, u32[]{:S(2)}) collective-permute-start(bf16[2,2,8,24,1536]{4,3,2,1,0:T(8,128)(2,1)} %pad_maximum_fusion.1), channel_id=1, source_target_pairs={{0,8},{8,16},{16,24},{1,9},{9,17},{17,25},{2,10},{10,18},{18,26},{... | collective-permute-start | bytes 7077896 | tf_op jit(solution)/shard_map/ppermute | solution.py:23
  37.5 28.9 %all-to-all-start = ((f32[32,2,4]{2,1,0:T(2,128)}), f32[32,2,4]{2,1,0:T(2,128)}, u32[]{:S(2)}, u32[]{:S(2)}) async-start(f32[32,2,4]{2,1,0:T(2,128)} %broadcast_in_dim.11), calls=%async_computation | async-start | bytes 65536 | tf_op jit(solution)/shard_map/all_to_all | solution.py:116
  69.9 19.5 %all-to-all-done = f32[32,2,4]{2,1,0:T(2,128)} async-done(((f32[32,2,4]{2,1,0:T(2,128)}), f32[32,2,4]{2,1,0:T(2,128)}, u32[]{:S(2)}, u32[]{:S(2)}) %all-to-all-start) | async-done | bytes 1056 | tf_op jit(solution)/shard_map/all_to_all | solution.py:116
  98.3 3.9 %fusion.12 = f32[1,2,24,24,1536]{4,3,2,1,0:T(8,128)} fusion(bf16[2,2,24,24,1536]{4,3,2,1,0:T(8,128)(2,1)S(1)} %pad_maximum_fusion), kind=kLoop, calls=%fused_computation.21 | loop fusion | flops 3538944 | bytes 10616832 | tf_op jit(solution)/shard_map/mul | solution.py:48
  102.2 5.1 %slice_convert_fusion = (f32[1,2,24,24,1536]{4,3,2,1,0:T(8,128)}, bf16[1,2,24,24,1536]{4,3,2,1,0:T(8,128)(2,1)}) fusion(bf16[2,2,24,24,1536]{4,3,2,1,0:T(8,128)(2,1)S(1)} %pad_maximum_fusion), kind=kLoop, calls=%fused_computation.8 | loop fusion | flops 1769472 | bytes 17694720 | tf_op jit(solution)/shard_map/convert_element_type | solution.py:46
  107.3 9.1 %mul.194 = f32[2,24,24,12,128]{4,3,2,1,0:T(8,128)} reshape(f32[1,2,24,24,1536]{4,3,2,1,0:T(8,128)} %fusion.12) | data formatting | bytes 14155776 | tf_op jit(solution)/shard_map/mul | solution.py:48
  116.4 6.2 %reduce_sum.91 = f32[2,24,24,12]{3,2,1,0:T(8,128)S(1)} reduce(f32[2,24,24,12,128]{4,3,2,1,0:T(8,128)} %mul.194, f32[]{:T(128)} %constant.88.clone.1), dimensions={4}, to_apply=%region_1.0 | reduce | flops 1755648 | bytes 7133188 | tf_op jit(solution)/shard_map/reduce_sum | solution.py:48
  123.2 9.1 %reshape.207 = f32[2,576,12,128]{3,2,1,0:T(8,128)} reshape(f32[1,2,24,24,1536]{4,3,2,1,0:T(8,128)} %get-tuple-element.20) | data formatting | bytes 14155776 | tf_op jit(solution)/shard_map/convert_element_type | solution.py:46
  132.3 7.4 %reshape_squeeze.3 = bf16[2,576,12,128]{3,2,1,0:T(8,128)(2,1)} reshape(bf16[1,2,24,24,1536]{4,3,2,1,0:T(8,128)(2,1)} %get-tuple-element.21) | data formatting | bytes 7077888 | tf_op jit(solution)/shard_map/reshape;squeeze | solution.py:134
  139.7 8.1 %fusion.3 = (f32[2,12,64]{2,1,0:T(8,128)S(1)}, f32[2,12,64,576]{3,2,1,0:T(8,128)S(1)}) fusion(pred[12,576]{1,0:T(8,128)(4,1)S(1)} %copy-done.9, f32[2,576,12,128]{3,2,1,0:T(8,128)} %reshape.207, f32[128]{0:T(128)S(1)} %copy-done.11, f32[2,576,12]{1,2,0:T(8,128)S(1)} %reshape.210, f32[128]{0:T(128)S(1)} %copy-done.14, f32[2,64,12]{1,2,0:T(8,128)S(1)} %copy.59, ...), kind=kOutput, calls=%fused_computation.11 | convolution fusion | flops 235043328 | bytes 11478784 | tf_op jit(solution)/shard_map/vmap(qhc,mhc->hqm)/dot_general | solution.py:42
  154.3 7.3 %fusion = (f32[128]{0:T(128)S(1)}, f32[2,12,576,128]{3,2,1,0:T(8,128)}) fusion(f32[2,576,12,128]{3,2,1,0:T(8,128)S(1)} %bitcast.97, f32[2,576,12]{1,2,0:T(8,128)S(1)} %reshape.210, bf16[2,12,64,576]{3,2,1,0:T(8,128)(2,1)S(1)} %fusion.1, f32[128]{0:T(128)S(1)} %copy-done.14, f32[2,64,12]{1,2,0:T(8,128)S(1)} %copy.59, f32[2,64,12,128]{3,2,1,0:T(8,128)S(1)} %reshape.198), kind=kOutput, calls=%fused_computation.2 | convolution fusion | flops 234160000 | bytes 16774144 | tf_op jit(solution)/shard_map/vmap(hqm,qhc->hmc)/dot_general | solution.py:42
  161.6 5.8 %multiply_reduce_fusion.1 = (f32[128]{0:T(128)S(1)}, f32[2,64,12]{1,2,0:T(8,128)}, f32[2,12,128,64]{2,3,1,0:T(8,128)S(1)}) fusion(f32[2,64,12]{1,2,0:T(8,128)S(1)} %copy.59, f32[2,64,12,128]{3,2,1,0:T(8,128)S(1)} %reshape.198, f32[128]{0:T(128)S(1)} %copy-done.18, bf16[2,12,64,576]{3,2,1,0:T(8,128)(2,1)S(1)} %fusion.1, ...), kind=kOutput, calls=%fused_computation.47 | convolution fusion | flops 233175424 | bytes 10489344 | tf_op jit(solution)/shard_map/vmap(hqm,mhc->qhc)/dot_general | solution.py:42
  181.2 5.9 %collective-permute-start.6 = (f32[2,128]{1,0:T(2,128)S(1)}, f32[2,128]{1,0:T(2,128)S(1)}, u32[]{:S(2)}, u32[]{:S(2)}) collective-permute-start(f32[2,128]{1,0:T(2,128)S(1)} %fusion.70), channel_id=1, source_target_pairs={{0,4},{1,5},{2,6},{3,7},{4,0},{5,1},{6,2},{7,3},{8,12},{9,13},{10,... | collective-permute-start | bytes 3080 | tf_op jit(solution)/shard_map/ppermute | solution.py:36
  190.7 6.7 %fusion.19 = f32[2,12,576,128]{3,2,1,0:T(8,128)} fusion(bf16[2,64,12,128]{3,2,1,0:T(8,128)(2,1)S(1)} %reshape.200, f32[2,12,64,576]{3,2,1,0:T(8,128)} %copy-done.2, f32[2,12,64]{2,1,0:T(8,128)} %copy-done.15, pred[12,576]{1,0:T(8,128)(4,1)} %and_and_fusion), kind=kOutput, calls=%fused_computation.26 | convolution fusion | flops 230031360 | bytes 11023104 | tf_op jit(solution)/shard_map/vmap(hqm,qhc->hmc)/dot_general | solution.py:42
  209.6 4.1 %collective-permute-start.10 = (bf16[2,12,8,24,128]{4,3,2,1,0:T(8,128)(2,1)}, bf16[2,12,8,24,128]{4,3,2,1,0:T(8,128)(2,1)}, u32[]{:S(2)}, u32[]{:S(2)}) collective-permute-start(bf16[2,12,8,24,128]{4,3,2,1,0:T(8,128)(2,1)} %get-tuple-element.25), channel_id=1, source_target_pairs={{0,8},{8,16},{16,24},{1,9},{9,17},{17,25},{2,10},{10,18},{18,26},{... | collective-permute-start | bytes 3538952 | tf_op jit(solution)/shard_map/ppermute | solution.py:83
  215.1 4.1 %all-to-all-start.1 = ((f32[32,2,4]{2,1,0:T(2,128)}), f32[32,2,4]{2,1,0:T(2,128)S(1)}, u32[]{:S(2)}, u32[]{:S(2)}) async-start(f32[32,2,4]{2,1,0:T(2,128)} %copy.82), calls=%async_computation.1 | async-start | bytes 65536 | tf_op jit(solution)/shard_map/all_to_all | solution.py:150
  219.2 3.6 %convert.20 = bf16[2,12,24,24,128]{4,3,2,1,0:T(8,128)(2,1)S(1)} convert(f32[2,12,24,24,128]{4,3,2,1,0:T(8,128)} %bitcast.103) | non-fusion elementwise | flops 1769472 | bytes 10616832 | tf_op jit(solution)/shard_map/convert.5
  225.9 4.1 %collective-permute-start.14 = (bf16[2,12,8,24,128]{4,3,2,1,0:T(8,128)(2,1)}, bf16[2,12,8,24,128]{4,3,2,1,0:T(8,128)(2,1)}, u32[]{:S(2)}, u32[]{:S(2)}) collective-permute-start(bf16[2,12,8,24,128]{4,3,2,1,0:T(8,128)(2,1)} %get-tuple-element.23), channel_id=1, source_target_pairs={{0,8},{8,16},{16,24},{1,9},{9,17},{17,25},{2,10},{10,18},{18,26},{... | collective-permute-start | bytes 3538952 | tf_op jit(solution)/shard_map/ppermute | solution.py:83
  232.5 9.7 %all-to-all-done.1 = f32[32,2,4]{2,1,0:T(2,128)S(1)} async-done(((f32[32,2,4]{2,1,0:T(2,128)}), f32[32,2,4]{2,1,0:T(2,128)S(1)}, u32[]{:S(2)}, u32[]{:S(2)}) %all-to-all-start.1) | async-done | bytes 1056 | tf_op jit(solution)/shard_map/all_to_all | solution.py:150
  249.3 7.3 %collective-permute-start.12 = (bf16[2,12,8,8,128]{4,3,2,1,0:T(8,128)(2,1)S(1)}, bf16[2,12,8,8,128]{4,3,2,1,0:T(8,128)(2,1)S(1)}, u32[]{:S(2)}, u32[]{:S(2)}) collective-permute-start(bf16[2,12,8,8,128]{4,3,2,1,0:T(8,128)(2,1)S(1)} %get-tuple-element.29), channel_id=1, source_target_pairs={{0,1},{1,2},{2,3},{3,4},{4,5},{5,6},{6,7},{8,9},{9,10},{10,11},{11... | collective-permute-start | bytes 1179656 | tf_op jit(solution)/shard_map/ppermute | solution.py:83
  256.6 4.5 %fusion.60 = (bf16[2,12,8,24,128]{4,3,2,1,0:T(8,128)(2,1)S(1)}, f32[2,12,8,24,128]{4,3,2,1,0:T(8,128)}) fusion(bf16[2,12,8,24,128]{4,3,2,1,0:T(8,128)(2,1)} %collective-permute-done.14, bf16[2,12,8,24,128]{4,3,2,1,0:T(8,128)(2,1)} %collective-permute-done.13, f32[2,12,24,24,128]{4,3,2,1,0:T(8,128)} %bitcast.104), kind=kLoop, calls=%fused_computation.118 | loop fusion | flops 2949120 | bytes 8257536 | tf_op jit(solution)/shard_map/convert.3
  264.2 7.5 %collective-permute-start.16 = (bf16[2,12,8,8,128]{4,3,2,1,0:T(8,128)(2,1)}, bf16[2,12,8,8,128]{4,3,2,1,0:T(8,128)(2,1)}, u32[]{:S(2)}, u32[]{:S(2)}) collective-permute-start(bf16[2,12,8,8,128]{4,3,2,1,0:T(8,128)(2,1)} %get-tuple-element.27), channel_id=1, source_target_pairs={{0,1},{1,2},{2,3},{3,4},{4,5},{5,6},{6,7},{8,9},{9,10},{10,11},{11... | collective-permute-start | bytes 1179656 | tf_op jit(solution)/shard_map/ppermute | solution.py:83
  (139 shorter events, 86.5 us)
Async XLA Ops:
  0.7 65.7 %copy-start.4 = (bf16[2,8,8,1536]{3,2,1,0:T(8,128)(2,1)S(1)}, bf16[2,8,8,1536]{3,2,1,0:T(8,128)(2,1)}, u32[]{:S(2)}) copy-start(bf16[2,8,8,1536]{3,2,1,0:T(8,128)(2,1)} %param.7) | copy-start | bytes 1179652
  0.7 66.2 %copy-start.19 = (s32[12,2]{0,1:T(2,128)S(1)}, s32[12,2]{0,1:T(2,128)}, u32[]{:S(2)}) copy-start(s32[12,2]{0,1:T(2,128)} %param.13) | copy-start | bytes 292
  1.9 92.9 %copy-start = (bf16[2,8,8,1536]{3,2,1,0:T(8,128)(2,1)S(1)}, bf16[2,8,8,1536]{3,2,1,0:T(8,128)(2,1)}, u32[]{:S(2)}) copy-start(bf16[2,8,8,1536]{3,2,1,0:T(8,128)(2,1)} %param.8) | copy-start | bytes 1179652
  1.9 92.9 %copy-start.3 = (bf16[2,8,8,1536]{3,2,1,0:T(8,128)(2,1)S(1)}, bf16[2,8,8,1536]{3,2,1,0:T(8,128)(2,1)}, u32[]{:S(2)}) copy-start(bf16[2,8,8,1536]{3,2,1,0:T(8,128)(2,1)} %param.9) | copy-start | bytes 1179652
  1.9 24.9 %collective-permute-start.1 = (bf16[2,2,8,8,1536]{4,3,2,1,0:T(8,128)(2,1)S(1)}, bf16[2,2,8,8,1536]{4,3,2,1,0:T(8,128)(2,1)S(1)}, u32[]{:S(2)}, u32[]{:S(2)}) collective-permute-start(bf16[2,2,8,8,1536]{4,3,2,1,0:T(8,128)(2,1)S(1)} %pad_maximum_fusion.2), channel_id=1, source_target_pairs={{1,0},{2,1},{3,2},{4,3},{5,4},{6,5},{7,6},{9,8},{10,9},{11,10},{12... | collective-permute-start | bytes 2359304 | tf_op jit(solution)/shard_map/ppermute | solution.py:25
  4.8 23.2 %collective-permute-start = (bf16[2,2,8,8,1536]{4,3,2,1,0:T(8,128)(2,1)S(1)}, bf16[2,2,8,8,1536]{4,3,2,1,0:T(8,128)(2,1)S(1)}, u32[]{:S(2)}, u32[]{:S(2)}) collective-permute-start(bf16[2,2,8,8,1536]{4,3,2,1,0:T(8,128)(2,1)S(1)} %pad_maximum_fusion.2), channel_id=1, source_target_pairs={{0,1},{1,2},{2,3},{3,4},{4,5},{5,6},{6,7},{8,9},{9,10},{10,11},{11... | collective-permute-start | bytes 2359304 | tf_op jit(solution)/shard_map/ppermute | solution.py:23
  28.0 39.5 %copy-start.5 = (bf16[2,2,8,8,1536]{4,3,2,1,0:T(8,128)(2,1)}, bf16[2,2,8,8,1536]{4,3,2,1,0:T(8,128)(2,1)S(1)}, u32[]{:S(2)}) copy-start(bf16[2,2,8,8,1536]{4,3,2,1,0:T(8,128)(2,1)S(1)} %collective-permute-done) | copy-start | bytes 2359300
  31.1 63.7 %collective-permute-start.3 = (bf16[2,2,8,24,1536]{4,3,2,1,0:T(8,128)(2,1)}, bf16[2,2,8,24,1536]{4,3,2,1,0:T(8,128)(2,1)}, u32[]{:S(2)}, u32[]{:S(2)}) collective-permute-start(bf16[2,2,8,24,1536]{4,3,2,1,0:T(8,128)(2,1)} %pad_maximum_fusion.1), channel_id=1, source_target_pairs={{8,0},{16,8},{24,16},{9,1},{17,9},{25,17},{10,2},{18,10},{26,18},{... | collective-permute-start | bytes 7077896 | tf_op jit(solution)/shard_map/ppermute | solution.py:25
  32.4 62.4 %collective-permute-start.2 = (bf16[2,2,8,24,1536]{4,3,2,1,0:T(8,128)(2,1)}, bf16[2,2,8,24,1536]{4,3,2,1,0:T(8,128)(2,1)}, u32[]{:S(2)}, u32[]{:S(2)}) collective-permute-start(bf16[2,2,8,24,1536]{4,3,2,1,0:T(8,128)(2,1)} %pad_maximum_fusion.1), channel_id=1, source_target_pairs={{0,8},{8,16},{16,24},{1,9},{9,17},{17,25},{2,10},{10,18},{18,26},{... | collective-permute-start | bytes 7077896 | tf_op jit(solution)/shard_map/ppermute | solution.py:23
  37.5 51.9 %all-to-all-start = ((f32[32,2,4]{2,1,0:T(2,128)}), f32[32,2,4]{2,1,0:T(2,128)}, u32[]{:S(2)}, u32[]{:S(2)}) async-start(f32[32,2,4]{2,1,0:T(2,128)} %broadcast_in_dim.11), calls=%async_computation | async-start | bytes 65536 | tf_op jit(solution)/shard_map/all_to_all | solution.py:116
  167.4 5.5 %collective-permute-start.4 = (f32[2,128]{1,0:T(2,128)S(1)}, f32[2,128]{1,0:T(2,128)S(1)}, u32[]{:S(2)}, u32[]{:S(2)}) collective-permute-start(f32[2,128]{1,0:T(2,128)S(1)} %pad_maximum_fusion.4), channel_id=1, source_target_pairs={{0,1},{1,0},{2,3},{3,2},{4,5},{5,4},{6,7},{7,6},{8,9},{9,8},{10,11... | collective-permute-start | bytes 3080 | tf_op jit(solution)/shard_map/ppermute | solution.py:36
  173.5 7.0 %collective-permute-start.5 = (f32[2,128]{1,0:T(2,128)S(1)}, f32[2,128]{1,0:T(2,128)S(1)}, u32[]{:S(2)}, u32[]{:S(2)}) collective-permute-start(f32[2,128]{1,0:T(2,128)S(1)} %fusion.54), channel_id=1, source_target_pairs={{0,2},{1,3},{2,0},{3,1},{4,6},{5,7},{6,4},{7,5},{8,10},{9,11},{10,... | collective-permute-start | bytes 3080 | tf_op jit(solution)/shard_map/ppermute | solution.py:36
  181.2 7.5 %collective-permute-start.6 = (f32[2,128]{1,0:T(2,128)S(1)}, f32[2,128]{1,0:T(2,128)S(1)}, u32[]{:S(2)}, u32[]{:S(2)}) collective-permute-start(f32[2,128]{1,0:T(2,128)S(1)} %fusion.70), channel_id=1, source_target_pairs={{0,4},{1,5},{2,6},{3,7},{4,0},{5,1},{6,2},{7,3},{8,12},{9,13},{10,... | collective-permute-start | bytes 3080 | tf_op jit(solution)/shard_map/ppermute | solution.py:36
  188.6 8.7 %collective-permute-start.7 = (f32[2,128]{1,0:T(2,128)S(1)}, f32[2,128]{1,0:T(2,128)S(1)}, u32[]{:S(2)}, u32[]{:S(2)}) collective-permute-start(f32[2,128]{1,0:T(2,128)S(1)} %add.163), channel_id=1, source_target_pairs={{0,8},{8,0},{16,24},{24,16},{1,9},{9,1},{17,25},{25,17},{2,10},{10... | collective-permute-start | bytes 3080 | tf_op jit(solution)/shard_map/ppermute | solution.py:36
  197.4 5.5 %collective-permute-start.8 = (f32[2,128]{1,0:T(2,128)S(1)}, f32[2,128]{1,0:T(2,128)S(1)}, u32[]{:S(2)}, u32[]{:S(2)}) collective-permute-start(f32[2,128]{1,0:T(2,128)S(1)} %add.164), channel_id=1, source_target_pairs={{0,16},{8,24},{16,0},{24,8},{1,17},{9,25},{17,1},{25,9},{2,18},{10... | collective-permute-start | bytes 3080 | tf_op jit(solution)/shard_map/ppermute | solution.py:36
  208.3 34.5 %collective-permute-start.9 = (bf16[2,12,8,24,128]{4,3,2,1,0:T(8,128)(2,1)}, bf16[2,12,8,24,128]{4,3,2,1,0:T(8,128)(2,1)}, u32[]{:S(2)}, u32[]{:S(2)}) collective-permute-start(bf16[2,12,8,24,128]{4,3,2,1,0:T(8,128)(2,1)} %get-tuple-element.24), channel_id=1, source_target_pairs={{8,0},{16,8},{24,16},{9,1},{17,9},{25,17},{10,2},{18,10},{26,18},{... | collective-permute-start | bytes 3538952 | tf_op jit(solution)/shard_map/ppermute | solution.py:82
  209.6 33.2 %collective-permute-start.10 = (bf16[2,12,8,24,128]{4,3,2,1,0:T(8,128)(2,1)}, bf16[2,12,8,24,128]{4,3,2,1,0:T(8,128)(2,1)}, u32[]{:S(2)}, u32[]{:S(2)}) collective-permute-start(bf16[2,12,8,24,128]{4,3,2,1,0:T(8,128)(2,1)} %get-tuple-element.25), channel_id=1, source_target_pairs={{0,8},{8,16},{16,24},{1,9},{9,17},{17,25},{2,10},{10,18},{18,26},{... | collective-permute-start | bytes 3538952 | tf_op jit(solution)/shard_map/ppermute | solution.py:83
  215.1 27.1 %all-to-all-start.1 = ((f32[32,2,4]{2,1,0:T(2,128)}), f32[32,2,4]{2,1,0:T(2,128)S(1)}, u32[]{:S(2)}, u32[]{:S(2)}) async-start(f32[32,2,4]{2,1,0:T(2,128)} %copy.82), calls=%async_computation.1 | async-start | bytes 65536 | tf_op jit(solution)/shard_map/all_to_all | solution.py:150
  224.6 32.0 %collective-permute-start.13 = (bf16[2,12,8,24,128]{4,3,2,1,0:T(8,128)(2,1)}, bf16[2,12,8,24,128]{4,3,2,1,0:T(8,128)(2,1)}, u32[]{:S(2)}, u32[]{:S(2)}) collective-permute-start(bf16[2,12,8,24,128]{4,3,2,1,0:T(8,128)(2,1)} %get-tuple-element.22), channel_id=1, source_target_pairs={{8,0},{16,8},{24,16},{9,1},{17,9},{25,17},{10,2},{18,10},{26,18},{... | collective-permute-start | bytes 3538952 | tf_op jit(solution)/shard_map/ppermute | solution.py:82
  225.9 30.7 %collective-permute-start.14 = (bf16[2,12,8,24,128]{4,3,2,1,0:T(8,128)(2,1)}, bf16[2,12,8,24,128]{4,3,2,1,0:T(8,128)(2,1)}, u32[]{:S(2)}, u32[]{:S(2)}) collective-permute-start(bf16[2,12,8,24,128]{4,3,2,1,0:T(8,128)(2,1)} %get-tuple-element.23), channel_id=1, source_target_pairs={{0,8},{8,16},{16,24},{1,9},{9,17},{17,25},{2,10},{10,18},{18,26},{... | collective-permute-start | bytes 3538952 | tf_op jit(solution)/shard_map/ppermute | solution.py:83
  245.9 25.8 %collective-permute-start.11 = (bf16[2,12,8,8,128]{4,3,2,1,0:T(8,128)(2,1)S(1)}, bf16[2,12,8,8,128]{4,3,2,1,0:T(8,128)(2,1)S(1)}, u32[]{:S(2)}, u32[]{:S(2)}) collective-permute-start(bf16[2,12,8,8,128]{4,3,2,1,0:T(8,128)(2,1)S(1)} %get-tuple-element.28), channel_id=1, source_target_pairs={{1,0},{2,1},{3,2},{4,3},{5,4},{6,5},{7,6},{9,8},{10,9},{11,10},{12... | collective-permute-start | bytes 1179656 | tf_op jit(solution)/shard_map/ppermute | solution.py:82
  249.3 22.4 %collective-permute-start.12 = (bf16[2,12,8,8,128]{4,3,2,1,0:T(8,128)(2,1)S(1)}, bf16[2,12,8,8,128]{4,3,2,1,0:T(8,128)(2,1)S(1)}, u32[]{:S(2)}, u32[]{:S(2)}) collective-permute-start(bf16[2,12,8,8,128]{4,3,2,1,0:T(8,128)(2,1)S(1)} %get-tuple-element.29), channel_id=1, source_target_pairs={{0,1},{1,2},{2,3},{3,4},{4,5},{5,6},{6,7},{8,9},{9,10},{10,11},{11... | collective-permute-start | bytes 1179656 | tf_op jit(solution)/shard_map/ppermute | solution.py:83
  262.2 17.6 %collective-permute-start.15 = (bf16[2,12,8,8,128]{4,3,2,1,0:T(8,128)(2,1)}, bf16[2,12,8,8,128]{4,3,2,1,0:T(8,128)(2,1)}, u32[]{:S(2)}, u32[]{:S(2)}) collective-permute-start(bf16[2,12,8,8,128]{4,3,2,1,0:T(8,128)(2,1)} %get-tuple-element.26), channel_id=1, source_target_pairs={{1,0},{2,1},{3,2},{4,3},{5,4},{6,5},{7,6},{9,8},{10,9},{11,10},{12... | collective-permute-start | bytes 1179656 | tf_op jit(solution)/shard_map/ppermute | solution.py:82
  264.2 15.7 %collective-permute-start.16 = (bf16[2,12,8,8,128]{4,3,2,1,0:T(8,128)(2,1)}, bf16[2,12,8,8,128]{4,3,2,1,0:T(8,128)(2,1)}, u32[]{:S(2)}, u32[]{:S(2)}) collective-permute-start(bf16[2,12,8,8,128]{4,3,2,1,0:T(8,128)(2,1)} %get-tuple-element.27), channel_id=1, source_target_pairs={{0,1},{1,2},{2,3},{3,4},{4,5},{5,6},{6,7},{8,9},{9,10},{10,11},{11... | collective-permute-start | bytes 1179656 | tf_op jit(solution)/shard_map/ppermute | solution.py:83
  (20 other events, 235.8 us)

commit v4 on v2

--- a/solution.py
+++ b/solution.py
@@ -150,7 +150,6 @@
     k_part = jnp.sum(key_part * jnp.swapaxes(as_near(k_normed_near), 1, 2), axis=(0, 1, 2))
     gain_parts = jnp.stack([q_part, k_part])
     plane_sum = xor_sum(xor_sum(gain_parts, "tx"), "ty")
-    plane_sum, key_part, value_part = lax.optimization_barrier((plane_sum, key_part, value_part))
     owner_count = lax.axis_size("fsdp")
     pieces = plane_sum.reshape(2, owner_count, share_len).transpose(1, 0, 2)
     owned = lax.all_to_all(pieces, "fsdp", 0, 0, tiled=True).sum(axis=0)

time: 286 us -> 280 us (0.979)
  other arithmetic: 50.8 us -> 42.9 us
  matrix products: 33.6 us -> 26 us
  waiting for transfers between devices: 54.6 us -> 60.3 us
    all_to_all x1, waiting for transfers between devices: 9.72 us -> 22 us  [body(): owned = lax.all_to_all(pieces, 'fsdp', 0, 0, tiled=True).sum(axis=0)]
    dot_general x6, matrix products: 33.6 us -> 26 us  [product(): return jnp.einsum(form, left, right, preferred_element_type=jnp.float32)]
    another operation x4, other arithmetic: 14.6 us -> 8.6 us
    ppermute x5, waiting for transfers between devices: 8.83 us -> 3.7 us  [xor_sum(): lax.ppermute(cells, axis, [(i, i ^ step) for i in range(count)])]
  transfers between devices with their start and end apart: 19 -> 19, of which waited for: 8 -> 6; matrix products, arithmetic and copies ran while one was open for 17% -> 15% of each run, Pallas kernels for 0% -> 0%
where the time goes in v4:
time: 280 us; the launch traced here: 275 us
  starting transfers between devices  94.8 us (34%)
  waiting for transfers between devices  60.3 us (22%)
  local copies, waits for them, and re-layouts  50 us (18%)
  other arithmetic  42.9 us (15%)
  matrix products  26 us (9%)
    all_to_all x1, starting transfers between devices, body(): gathered_gains = lax.all_to_all(own_gains, 'fsdp', 0, 0, tiled=True)  28.9 us
    dot_general x6, matrix products, product(): return jnp.einsum(form, left, right, preferred_element_type=jnp.float32)  26 us
    ppermute x4, starting transfers between devices, gathered(): lax.ppermute(tail.astype(jnp.bfloat16), axis, [(i, (i + 1) % count) for i...  23.4 us
    all_to_all x1, waiting for transfers between devices, body(): owned = lax.all_to_all(pieces, 'fsdp', 0, 0, tiled=True).sum(axis=0)  22 us
    all_to_all x1, waiting for transfers between devices, body(): gathered_gains = lax.all_to_all(own_gains, 'fsdp', 0, 0, tiled=True)  18.2 us
    ppermute x5, starting transfers between devices, xor_sum(): lax.ppermute(cells, axis, [(i, i ^ step) for i in range(count)])  16.8 us
    ppermute x2, waiting for transfers between devices, padded(): lax.ppermute(head, axis, [((i + 1) % count, i) for i in range(ends)])  15.3 us
    ppermute x2, starting transfers between devices, padded(): lax.ppermute(tail, axis, [(i, (i + 1) % count) for i in range(ends)])  11.2 us
  transfers between devices with their start and end apart: 19, of which 6 were waited for; matrix products, arithmetic and copies ran while one was open for 15% of the time, Pallas kernels for 0%

profile of v4, /device:TPU:6, one launch (start us, length us, event | category | flops | bytes accessed | tf_op | source)
XLA Modules:
  0.0 275.2 jit_solution(17323967125502568308)
XLA Ops:
  4.8 6.7 %collective-permute-start = (bf16[2,2,8,8,1536]{4,3,2,1,0:T(8,128)(2,1)S(1)}, bf16[2,2,8,8,1536]{4,3,2,1,0:T(8,128)(2,1)S(1)}, u32[]{:S(2)}, u32[]{:S(2)}) collective-permute-start(bf16[2,2,8,8,1536]{4,3,2,1,0:T(8,128)(2,1)S(1)} %pad_maximum_fusion.2), channel_id=1, source_target_pairs={{0,1},{1,2},{2,3},{3,4},{4,5},{5,6},{6,7},{8,9},{9,10},{10,11},{11... | collective-permute-start | bytes 2359304 | tf_op jit(solution)/shard_map/ppermute | solution.py:22
  11.6 15.3 %collective-permute-done.1 = bf16[2,2,8,8,1536]{4,3,2,1,0:T(8,128)(2,1)S(1)} collective-permute-done((bf16[2,2,8,8,1536]{4,3,2,1,0:T(8,128)(2,1)S(1)}, bf16[2,2,8,8,1536]{4,3,2,1,0:T(8,128)(2,1)S(1)}, u32[]{:S(2)}, u32[]{:S(2)}) %collective-permute-start.1) | collective-permute-done | bytes 786464 | tf_op jit(solution)/shard_map/ppermute | solution.py:24
  32.4 4.5 %collective-permute-start.2 = (bf16[2,2,8,24,1536]{4,3,2,1,0:T(8,128)(2,1)}, bf16[2,2,8,24,1536]{4,3,2,1,0:T(8,128)(2,1)}, u32[]{:S(2)}, u32[]{:S(2)}) collective-permute-start(bf16[2,2,8,24,1536]{4,3,2,1,0:T(8,128)(2,1)} %pad_maximum_fusion.1), channel_id=1, source_target_pairs={{0,8},{8,16},{16,24},{1,9},{9,17},{17,25},{2,10},{10,18},{18,26},{... | collective-permute-start | bytes 7077896 | tf_op jit(solution)/shard_map/ppermute | solution.py:22
  37.5 28.9 %all-to-all-start = ((f32[32,2,4]{2,1,0:T(2,128)}), f32[32,2,4]{2,1,0:T(2,128)}, u32[]{:S(2)}, u32[]{:S(2)}) async-start(f32[32,2,4]{2,1,0:T(2,128)} %broadcast_in_dim.11), calls=%async_computation | async-start | bytes 65536 | tf_op jit(solution)/shard_map/all_to_all | solution.py:122
  71.3 18.2 %all-to-all-done = f32[32,2,4]{2,1,0:T(2,128)} async-done(((f32[32,2,4]{2,1,0:T(2,128)}), f32[32,2,4]{2,1,0:T(2,128)}, u32[]{:S(2)}, u32[]{:S(2)}) %all-to-all-start) | async-done | bytes 1056 | tf_op jit(solution)/shard_map/all_to_all | solution.py:122
  96.2 3.5 %pad_maximum_fusion = bf16[2,2,24,24,1536]{4,3,2,1,0:T(8,128)(2,1)S(1)} fusion(bf16[2,2,8,24,1536]{4,3,2,1,0:T(8,128)(2,1)} %collective-permute-done.3, bf16[2,2,8,8,1536]{4,3,2,1,0:T(8,128)(2,1)S(1)} %collective-permute-done.1, bf16[1,2,8,8,1536]{4,3,2,1,0:T(8,128)(2,1)S(1)} %bitcast.107, bf16[1,2,8,8,1536]{4,3,2,1,0:T(8,128)(2,1)S(1)} %bitcast.102, ...), kind=kLoop, calls=%fused_computation | loop fusion | flops 42467328 | bytes 14155776 | tf_op jit(solution)/shard_map/concatenate | solution.py:20
  99.7 3.9 %fusion.12 = f32[1,2,24,24,1536]{4,3,2,1,0:T(8,128)} fusion(bf16[2,2,24,24,1536]{4,3,2,1,0:T(8,128)(2,1)S(1)} %pad_maximum_fusion), kind=kLoop, calls=%fused_computation.21 | loop fusion | flops 3538944 | bytes 10616832 | tf_op jit(solution)/shard_map/mul | solution.py:47
  103.6 5.1 %slice_convert_fusion = (f32[1,2,24,24,1536]{4,3,2,1,0:T(8,128)}, bf16[1,2,24,24,1536]{4,3,2,1,0:T(8,128)(2,1)}) fusion(bf16[2,2,24,24,1536]{4,3,2,1,0:T(8,128)(2,1)S(1)} %pad_maximum_fusion), kind=kLoop, calls=%fused_computation.8 | loop fusion | flops 1769472 | bytes 17694720 | tf_op jit(solution)/shard_map/convert_element_type | solution.py:45
  108.7 9.1 %mul.194 = f32[2,24,24,12,128]{4,3,2,1,0:T(8,128)} reshape(f32[1,2,24,24,1536]{4,3,2,1,0:T(8,128)} %fusion.12) | data formatting | bytes 14155776 | tf_op jit(solution)/shard_map/mul | solution.py:47
  117.8 6.2 %reduce_sum.91 = f32[2,24,24,12]{3,2,1,0:T(8,128)S(1)} reduce(f32[2,24,24,12,128]{4,3,2,1,0:T(8,128)} %mul.194, f32[]{:T(128)} %constant.88.clone.1), dimensions={4}, to_apply=%region_1.0 | reduce | flops 1755648 | bytes 7133188 | tf_op jit(solution)/shard_map/reduce_sum | solution.py:47
  124.6 9.1 %reshape.207 = f32[2,576,12,128]{3,2,1,0:T(8,128)} reshape(f32[1,2,24,24,1536]{4,3,2,1,0:T(8,128)} %get-tuple-element.14) | data formatting | bytes 14155776 | tf_op jit(solution)/shard_map/convert_element_type | solution.py:45
  133.7 7.4 %reshape_squeeze.3 = bf16[2,576,12,128]{3,2,1,0:T(8,128)(2,1)} reshape(bf16[1,2,24,24,1536]{4,3,2,1,0:T(8,128)(2,1)} %get-tuple-element.15) | data formatting | bytes 7077888 | tf_op jit(solution)/shard_map/reshape;squeeze | solution.py:140
  141.1 8.2 %fusion.3 = (f32[2,12,64]{2,1,0:T(8,128)S(1)}, f32[2,12,64,576]{3,2,1,0:T(8,128)S(1)}) fusion(pred[12,576]{1,0:T(8,128)(4,1)S(1)} %copy-done.9, f32[2,576,12,128]{3,2,1,0:T(8,128)} %reshape.207, f32[128]{0:T(128)S(1)} %copy-done.11, f32[2,576,12]{1,2,0:T(8,128)S(1)} %reshape.210, f32[128]{0:T(128)S(1)} %copy-done.13, f32[2,64,12]{1,2,0:T(8,128)S(1)} %copy.59, ...), kind=kOutput, calls=%fused_computation.11 | convolution fusion | flops 235043328 | bytes 11478784 | tf_op jit(solution)/shard_map/vmap(qhc,mhc->hqm)/dot_general | solution.py:41
  152.3 3.1 %fusion.1 = bf16[2,12,64,576]{3,2,1,0:T(8,128)(2,1)S(1)} fusion(f32[2,12,64]{2,1,0:T(8,128)S(1)} %bitcast.109, bf16[2,576,12,128]{3,2,1,0:T(8,128)(2,1)S(1)} %copy-done.3, bf16[2,64,12,128]{3,2,1,0:T(8,128)(2,1)S(1)} %reshape.200, f32[2,12,64]{2,1,0:T(8,128)S(1)} %get-tuple-element.30, f32[2,12,64,576]{3,2,1,0:T(8,128)S(1)} %get-tuple-element.31, ...), kind=kOutput, calls=%fused_computation.6 | convolution fusion | flops 231800832 | bytes 9259776 | tf_op jit(solution)/shard_map/vmap(qhc,mhc->hqm)/dot_general | solution.py:41
  155.7 5.7 %fusion = (f32[128]{0:T(128)S(1)}, f32[2,12,576,128]{3,2,1,0:T(8,128)S(1)}) fusion(f32[2,576,12,128]{3,2,1,0:T(8,128)S(1)} %bitcast.97, f32[2,576,12]{1,2,0:T(8,128)S(1)} %reshape.210, bf16[2,12,64,576]{3,2,1,0:T(8,128)(2,1)S(1)} %fusion.1, f32[128]{0:T(128)S(1)} %copy-done.13, f32[2,64,12]{1,2,0:T(8,128)S(1)} %copy.59, f32[2,64,12,128]{3,2,1,0:T(8,128)S(1)} %reshape.198), kind=kOutput, calls=%fused_computation.2 | convolution fusion | flops 234160000 | bytes 16774144 | tf_op jit(solution)/shard_map/vmap(hqm,qhc->hmc)/dot_general | solution.py:41
  161.4 4.6 %multiply_reduce_fusion = (f32[128]{0:T(128)S(1)}, f32[2,64,12]{1,2,0:T(8,128)S(1)}, f32[2,12,128,64]{2,3,1,0:T(8,128)S(1)}) fusion(f32[2,64,12]{1,2,0:T(8,128)S(1)} %copy.59, f32[2,64,12,128]{3,2,1,0:T(8,128)S(1)} %reshape.198, f32[128]{0:T(128)S(1)} %copy-done.14, bf16[2,12,64,576]{3,2,1,0:T(8,128)(2,1)S(1)} %fusion.1, ...), kind=kOutput, calls=%fused_computation.45 | convolution fusion | flops 233175424 | bytes 10489344 | tf_op jit(solution)/shard_map/vmap(hqm,mhc->qhc)/dot_general | solution.py:41
  179.8 7.9 %collective-permute-start.14 = (f32[2,128]{1,0:T(2,128)S(1)}, f32[2,128]{1,0:T(2,128)S(1)}, u32[]{:S(2)}, u32[]{:S(2)}) collective-permute-start(f32[2,128]{1,0:T(2,128)S(1)} %fusion.70), channel_id=1, source_target_pairs={{0,4},{1,5},{2,6},{3,7},{4,0},{5,1},{6,2},{7,3},{8,12},{9,13},{10,... | collective-permute-start | bytes 3080 | tf_op jit(solution)/shard_map/ppermute | solution.py:35
  191.0 4.1 %collective-permute-start.5 = (bf16[2,12,8,24,128]{4,3,2,1,0:T(8,128)(2,1)}, bf16[2,12,8,24,128]{4,3,2,1,0:T(8,128)(2,1)}, u32[]{:S(2)}, u32[]{:S(2)}) collective-permute-start(bf16[2,12,8,24,128]{4,3,2,1,0:T(8,128)(2,1)} %get-tuple-element.19), channel_id=1, source_target_pairs={{0,8},{8,16},{16,24},{1,9},{9,17},{17,25},{2,10},{10,18},{18,26},{... | collective-permute-start | bytes 3538952 | tf_op jit(solution)/shard_map/ppermute | solution.py:89
  203.1 4.1 %collective-permute-start.9 = (bf16[2,12,8,24,128]{4,3,2,1,0:T(8,128)(2,1)}, bf16[2,12,8,24,128]{4,3,2,1,0:T(8,128)(2,1)}, u32[]{:S(2)}, u32[]{:S(2)}) collective-permute-start(bf16[2,12,8,24,128]{4,3,2,1,0:T(8,128)(2,1)} %get-tuple-element.17), channel_id=1, source_target_pairs={{0,8},{8,16},{16,24},{1,9},{9,17},{17,25},{2,10},{10,18},{18,26},{... | collective-permute-start | bytes 3538952 | tf_op jit(solution)/shard_map/ppermute | solution.py:89
  208.0 3.9 %all-to-all-start.1 = ((f32[32,2,4]{2,1,0:T(2,128)}), f32[32,2,4]{2,1,0:T(2,128)S(1)}, u32[]{:S(2)}, u32[]{:S(2)}) async-start(f32[32,2,4]{2,1,0:T(2,128)} %copy.82), calls=%async_computation.1 | async-start | bytes 65536 | tf_op jit(solution)/shard_map/all_to_all | solution.py:155
  214.4 22.0 %all-to-all-done.1 = f32[32,2,4]{2,1,0:T(2,128)S(1)} async-done(((f32[32,2,4]{2,1,0:T(2,128)}), f32[32,2,4]{2,1,0:T(2,128)S(1)}, u32[]{:S(2)}, u32[]{:S(2)}) %all-to-all-start.1) | async-done | bytes 1056 | tf_op jit(solution)/shard_map/all_to_all | solution.py:155
  242.0 7.7 %collective-permute-start.7 = (bf16[2,12,8,8,128]{4,3,2,1,0:T(8,128)(2,1)S(1)}, bf16[2,12,8,8,128]{4,3,2,1,0:T(8,128)(2,1)S(1)}, u32[]{:S(2)}, u32[]{:S(2)}) collective-permute-start(bf16[2,12,8,8,128]{4,3,2,1,0:T(8,128)(2,1)S(1)} %get-tuple-element.23), channel_id=1, source_target_pairs={{0,1},{1,2},{2,3},{3,4},{4,5},{5,6},{6,7},{8,9},{9,10},{10,11},{11... | collective-permute-start | bytes 1179656 | tf_op jit(solution)/shard_map/ppermute | solution.py:89
  249.7 4.5 %fusion.60 = (bf16[2,12,8,24,128]{4,3,2,1,0:T(8,128)(2,1)S(1)}, f32[2,12,8,24,128]{4,3,2,1,0:T(8,128)}) fusion(bf16[2,12,8,24,128]{4,3,2,1,0:T(8,128)(2,1)} %collective-permute-done.9, bf16[2,12,8,24,128]{4,3,2,1,0:T(8,128)(2,1)} %collective-permute-done.8, f32[2,12,24,24,128]{4,3,2,1,0:T(8,128)} %bitcast.104), kind=kLoop, calls=%fused_computation.118 | loop fusion | flops 2949120 | bytes 8257536 | tf_op jit(solution)/shard_map/convert.3
  257.2 7.5 %collective-permute-start.11 = (bf16[2,12,8,8,128]{4,3,2,1,0:T(8,128)(2,1)}, bf16[2,12,8,8,128]{4,3,2,1,0:T(8,128)(2,1)}, u32[]{:S(2)}, u32[]{:S(2)}) collective-permute-start(bf16[2,12,8,8,128]{4,3,2,1,0:T(8,128)(2,1)} %get-tuple-element.21), channel_id=1, source_target_pairs={{0,1},{1,2},{2,3},{3,4},{4,5},{5,6},{6,7},{8,9},{9,10},{10,11},{11... | collective-permute-start | bytes 1179656 | tf_op jit(solution)/shard_map/ppermute | solution.py:89
  (131 shorter events, 73.1 us)
Async XLA Ops:
  0.6 66.2 %copy-start.1 = (bf16[2,8,8,1536]{3,2,1,0:T(8,128)(2,1)S(1)}, bf16[2,8,8,1536]{3,2,1,0:T(8,128)(2,1)}, u32[]{:S(2)}) copy-start(bf16[2,8,8,1536]{3,2,1,0:T(8,128)(2,1)} %param.8) | copy-start | bytes 1179652
  0.7 65.7 %copy-start.5 = (bf16[2,8,8,1536]{3,2,1,0:T(8,128)(2,1)S(1)}, bf16[2,8,8,1536]{3,2,1,0:T(8,128)(2,1)}, u32[]{:S(2)}) copy-start(bf16[2,8,8,1536]{3,2,1,0:T(8,128)(2,1)} %param.7) | copy-start | bytes 1179652
  0.7 66.7 %copy-start.15 = (s32[12,2]{0,1:T(2,128)S(1)}, s32[12,2]{0,1:T(2,128)}, u32[]{:S(2)}) copy-start(s32[12,2]{0,1:T(2,128)} %param.13) | copy-start | bytes 292
  1.9 94.3 %copy-start.4 = (bf16[2,8,8,1536]{3,2,1,0:T(8,128)(2,1)S(1)}, bf16[2,8,8,1536]{3,2,1,0:T(8,128)(2,1)}, u32[]{:S(2)}) copy-start(bf16[2,8,8,1536]{3,2,1,0:T(8,128)(2,1)} %param.9) | copy-start | bytes 1179652
  2.0 24.9 %collective-permute-start.1 = (bf16[2,2,8,8,1536]{4,3,2,1,0:T(8,128)(2,1)S(1)}, bf16[2,2,8,8,1536]{4,3,2,1,0:T(8,128)(2,1)S(1)}, u32[]{:S(2)}, u32[]{:S(2)}) collective-permute-start(bf16[2,2,8,8,1536]{4,3,2,1,0:T(8,128)(2,1)S(1)} %pad_maximum_fusion.2), channel_id=1, source_target_pairs={{1,0},{2,1},{3,2},{4,3},{5,4},{6,5},{7,6},{9,8},{10,9},{11,10},{12... | collective-permute-start | bytes 2359304 | tf_op jit(solution)/shard_map/ppermute | solution.py:24
  4.8 23.2 %collective-permute-start = (bf16[2,2,8,8,1536]{4,3,2,1,0:T(8,128)(2,1)S(1)}, bf16[2,2,8,8,1536]{4,3,2,1,0:T(8,128)(2,1)S(1)}, u32[]{:S(2)}, u32[]{:S(2)}) collective-permute-start(bf16[2,2,8,8,1536]{4,3,2,1,0:T(8,128)(2,1)S(1)} %pad_maximum_fusion.2), channel_id=1, source_target_pairs={{0,1},{1,2},{2,3},{3,4},{4,5},{5,6},{6,7},{8,9},{9,10},{10,11},{11... | collective-permute-start | bytes 2359304 | tf_op jit(solution)/shard_map/ppermute | solution.py:22
  28.1 39.4 %copy-start.6 = (bf16[2,2,8,8,1536]{4,3,2,1,0:T(8,128)(2,1)}, bf16[2,2,8,8,1536]{4,3,2,1,0:T(8,128)(2,1)S(1)}, u32[]{:S(2)}) copy-start(bf16[2,2,8,8,1536]{4,3,2,1,0:T(8,128)(2,1)S(1)} %collective-permute-done) | copy-start | bytes 2359300
  31.1 65.1 %collective-permute-start.3 = (bf16[2,2,8,24,1536]{4,3,2,1,0:T(8,128)(2,1)}, bf16[2,2,8,24,1536]{4,3,2,1,0:T(8,128)(2,1)}, u32[]{:S(2)}, u32[]{:S(2)}) collective-permute-start(bf16[2,2,8,24,1536]{4,3,2,1,0:T(8,128)(2,1)} %pad_maximum_fusion.1), channel_id=1, source_target_pairs={{8,0},{16,8},{24,16},{9,1},{17,9},{25,17},{10,2},{18,10},{26,18},{... | collective-permute-start | bytes 7077896 | tf_op jit(solution)/shard_map/ppermute | solution.py:24
  32.4 63.8 %collective-permute-start.2 = (bf16[2,2,8,24,1536]{4,3,2,1,0:T(8,128)(2,1)}, bf16[2,2,8,24,1536]{4,3,2,1,0:T(8,128)(2,1)}, u32[]{:S(2)}, u32[]{:S(2)}) collective-permute-start(bf16[2,2,8,24,1536]{4,3,2,1,0:T(8,128)(2,1)} %pad_maximum_fusion.1), channel_id=1, source_target_pairs={{0,8},{8,16},{16,24},{1,9},{9,17},{17,25},{2,10},{10,18},{18,26},{... | collective-permute-start | bytes 7077896 | tf_op jit(solution)/shard_map/ppermute | solution.py:22
  37.5 52.0 %all-to-all-start = ((f32[32,2,4]{2,1,0:T(2,128)}), f32[32,2,4]{2,1,0:T(2,128)}, u32[]{:S(2)}, u32[]{:S(2)}) async-start(f32[32,2,4]{2,1,0:T(2,128)} %broadcast_in_dim.11), calls=%async_computation | async-start | bytes 65536 | tf_op jit(solution)/shard_map/all_to_all | solution.py:122
  166.0 6.8 %collective-permute-start.12 = (f32[2,128]{1,0:T(2,128)S(1)}, f32[2,128]{1,0:T(2,128)S(1)}, u32[]{:S(2)}, u32[]{:S(2)}) collective-permute-start(f32[2,128]{1,0:T(2,128)S(1)} %pad_maximum_fusion.4), channel_id=1, source_target_pairs={{0,1},{1,0},{2,3},{3,2},{4,5},{5,4},{6,7},{7,6},{8,9},{9,8},{10,11... | collective-permute-start | bytes 3080 | tf_op jit(solution)/shard_map/ppermute | solution.py:35
  172.8 7.0 %collective-permute-start.13 = (f32[2,128]{1,0:T(2,128)S(1)}, f32[2,128]{1,0:T(2,128)S(1)}, u32[]{:S(2)}, u32[]{:S(2)}) collective-permute-start(f32[2,128]{1,0:T(2,128)S(1)} %fusion.54), channel_id=1, source_target_pairs={{0,2},{1,3},{2,0},{3,1},{4,6},{5,7},{6,4},{7,5},{8,10},{9,11},{10,... | collective-permute-start | bytes 3080 | tf_op jit(solution)/shard_map/ppermute | solution.py:35
  179.8 15.2 %collective-permute-start.14 = (f32[2,128]{1,0:T(2,128)S(1)}, f32[2,128]{1,0:T(2,128)S(1)}, u32[]{:S(2)}, u32[]{:S(2)}) collective-permute-start(f32[2,128]{1,0:T(2,128)S(1)} %fusion.70), channel_id=1, source_target_pairs={{0,4},{1,5},{2,6},{3,7},{4,0},{5,1},{6,2},{7,3},{8,12},{9,13},{10,... | collective-permute-start | bytes 3080 | tf_op jit(solution)/shard_map/ppermute | solution.py:35
  189.5 47.4 %collective-permute-start.4 = (bf16[2,12,8,24,128]{4,3,2,1,0:T(8,128)(2,1)}, bf16[2,12,8,24,128]{4,3,2,1,0:T(8,128)(2,1)}, u32[]{:S(2)}, u32[]{:S(2)}) collective-permute-start(bf16[2,12,8,24,128]{4,3,2,1,0:T(8,128)(2,1)} %get-tuple-element.18), channel_id=1, source_target_pairs={{8,0},{16,8},{24,16},{9,1},{17,9},{25,17},{10,2},{18,10},{26,18},{... | collective-permute-start | bytes 3538952 | tf_op jit(solution)/shard_map/ppermute | solution.py:88
  191.0 45.9 %collective-permute-start.5 = (bf16[2,12,8,24,128]{4,3,2,1,0:T(8,128)(2,1)}, bf16[2,12,8,24,128]{4,3,2,1,0:T(8,128)(2,1)}, u32[]{:S(2)}, u32[]{:S(2)}) collective-permute-start(bf16[2,12,8,24,128]{4,3,2,1,0:T(8,128)(2,1)} %get-tuple-element.19), channel_id=1, source_target_pairs={{0,8},{8,16},{16,24},{1,9},{9,17},{17,25},{2,10},{10,18},{18,26},{... | collective-permute-start | bytes 3538952 | tf_op jit(solution)/shard_map/ppermute | solution.py:89
  195.0 3.0 %collective-permute-start.15 = (f32[2,128]{1,0:T(2,128)S(1)}, f32[2,128]{1,0:T(2,128)S(1)}, u32[]{:S(2)}, u32[]{:S(2)}) collective-permute-start(f32[2,128]{1,0:T(2,128)S(1)} %add.171), channel_id=1, source_target_pairs={{0,8},{8,0},{16,24},{24,16},{1,9},{9,1},{17,25},{25,17},{2,10},{10... | collective-permute-start | bytes 3080 | tf_op jit(solution)/shard_map/ppermute | solution.py:35
  198.1 9.1 %collective-permute-start.16 = (f32[2,128]{1,0:T(2,128)S(1)}, f32[2,128]{1,0:T(2,128)S(1)}, u32[]{:S(2)}, u32[]{:S(2)}) collective-permute-start(f32[2,128]{1,0:T(2,128)S(1)} %add.172), channel_id=1, source_target_pairs={{0,16},{8,24},{16,0},{24,8},{1,17},{9,25},{17,1},{25,9},{2,18},{10... | collective-permute-start | bytes 3080 | tf_op jit(solution)/shard_map/ppermute | solution.py:35
  201.8 47.9 %collective-permute-start.8 = (bf16[2,12,8,24,128]{4,3,2,1,0:T(8,128)(2,1)}, bf16[2,12,8,24,128]{4,3,2,1,0:T(8,128)(2,1)}, u32[]{:S(2)}, u32[]{:S(2)}) collective-permute-start(bf16[2,12,8,24,128]{4,3,2,1,0:T(8,128)(2,1)} %get-tuple-element.16), channel_id=1, source_target_pairs={{8,0},{16,8},{24,16},{9,1},{17,9},{25,17},{10,2},{18,10},{26,18},{... | collective-permute-start | bytes 3538952 | tf_op jit(solution)/shard_map/ppermute | solution.py:88
  203.1 46.6 %collective-permute-start.9 = (bf16[2,12,8,24,128]{4,3,2,1,0:T(8,128)(2,1)}, bf16[2,12,8,24,128]{4,3,2,1,0:T(8,128)(2,1)}, u32[]{:S(2)}, u32[]{:S(2)}) collective-permute-start(bf16[2,12,8,24,128]{4,3,2,1,0:T(8,128)(2,1)} %get-tuple-element.17), channel_id=1, source_target_pairs={{0,8},{8,16},{16,24},{1,9},{9,17},{17,25},{2,10},{10,18},{18,26},{... | collective-permute-start | bytes 3538952 | tf_op jit(solution)/shard_map/ppermute | solution.py:89
  208.0 28.4 %all-to-all-start.1 = ((f32[32,2,4]{2,1,0:T(2,128)}), f32[32,2,4]{2,1,0:T(2,128)S(1)}, u32[]{:S(2)}, u32[]{:S(2)}) async-start(f32[32,2,4]{2,1,0:T(2,128)} %copy.82), calls=%async_computation.1 | async-start | bytes 65536 | tf_op jit(solution)/shard_map/all_to_all | solution.py:155
  240.1 24.7 %collective-permute-start.6 = (bf16[2,12,8,8,128]{4,3,2,1,0:T(8,128)(2,1)S(1)}, bf16[2,12,8,8,128]{4,3,2,1,0:T(8,128)(2,1)S(1)}, u32[]{:S(2)}, u32[]{:S(2)}) collective-permute-start(bf16[2,12,8,8,128]{4,3,2,1,0:T(8,128)(2,1)S(1)} %get-tuple-element.22), channel_id=1, source_target_pairs={{1,0},{2,1},{3,2},{4,3},{5,4},{6,5},{7,6},{9,8},{10,9},{11,10},{12... | collective-permute-start | bytes 1179656 | tf_op jit(solution)/shard_map/ppermute | solution.py:88
  242.0 22.8 %collective-permute-start.7 = (bf16[2,12,8,8,128]{4,3,2,1,0:T(8,128)(2,1)S(1)}, bf16[2,12,8,8,128]{4,3,2,1,0:T(8,128)(2,1)S(1)}, u32[]{:S(2)}, u32[]{:S(2)}) collective-permute-start(bf16[2,12,8,8,128]{4,3,2,1,0:T(8,128)(2,1)S(1)} %get-tuple-element.23), channel_id=1, source_target_pairs={{0,1},{1,2},{2,3},{3,4},{4,5},{5,6},{6,7},{8,9},{9,10},{10,11},{11... | collective-permute-start | bytes 1179656 | tf_op jit(solution)/shard_map/ppermute | solution.py:89
  255.3 17.6 %collective-permute-start.10 = (bf16[2,12,8,8,128]{4,3,2,1,0:T(8,128)(2,1)}, bf16[2,12,8,8,128]{4,3,2,1,0:T(8,128)(2,1)}, u32[]{:S(2)}, u32[]{:S(2)}) collective-permute-start(bf16[2,12,8,8,128]{4,3,2,1,0:T(8,128)(2,1)} %get-tuple-element.20), channel_id=1, source_target_pairs={{1,0},{2,1},{3,2},{4,3},{5,4},{6,5},{7,6},{9,8},{10,9},{11,10},{12... | collective-permute-start | bytes 1179656 | tf_op jit(solution)/shard_map/ppermute | solution.py:88
  257.2 15.7 %collective-permute-start.11 = (bf16[2,12,8,8,128]{4,3,2,1,0:T(8,128)(2,1)}, bf16[2,12,8,8,128]{4,3,2,1,0:T(8,128)(2,1)}, u32[]{:S(2)}, u32[]{:S(2)}) collective-permute-start(bf16[2,12,8,8,128]{4,3,2,1,0:T(8,128)(2,1)} %get-tuple-element.21), channel_id=1, source_target_pairs={{0,1},{1,2},{2,3},{3,4},{4,5},{5,6},{6,7},{8,9},{9,10},{10,11},{11... | collective-permute-start | bytes 1179656 | tf_op jit(solution)/shard_map/ppermute | solution.py:89
  (16 other events, 226.8 us)
